TPU v7x, 32 devices: a whole 2x2x4 slice. The times are simulated.
32 devices in a mesh: rep: 2 (over y), ctx: 8 (over z, x), head: 2 (over core).
Axes of the slice: x: 2, y: 2, z: 4, core: 2. Of those that a mesh axis runs over, the one named last changes fastest.
Arguments:
- queries: bfloat16 [1024, 32, 128], P(('rep', 'ctx'), 'head'), parts along dimension 0, may hold values from -6 to 6
- keys: bfloat16 [1024, 4, 128], P(('rep', 'ctx'), 'head'), parts along dimension 0, may hold values from -6 to 6
- values: bfloat16 [1024, 4, 128], P(('rep', 'ctx'), 'head'), parts along dimension 0, may hold values from -6 to 6
Outputs:
- attended: bfloat16 [1024, 32, 128], P(('rep', 'ctx'), 'head'), parts along dimension 0
There are 2 independent parts, one for each index of `rep`. A program takes and returns all parts, laid end to end along the dimension named above; each array names one. Nothing has to cross between parts.
All inputs are finite; a program needn't handle non-finite values.
Results may differ from a plain program's by a relative error of at most 0.0037.
Values may be sent and summed in bfloat16 or wider, within the bound.
No kernel may reach another device: no remote copies, remote signals or barrier semaphores. Data moves between devices by JAX's collectives and lax.ppermute only.
A program may use at most 128 MiB of HBM per device.

v0:
```python
import jax
import jax.numpy as jnp
from jax import lax
from jax.sharding import PartitionSpec as P


def from_partner(x, axis, bit):
    return lax.ppermute(x, axis, [(i, i ^ 1 << bit) for i in range(lax.axis_size(axis))])


def attend_piece(state, rows, position, key_piece, value_piece, scale):
    running_max, running_sum, weighted = state
    scores = (
        jnp.einsum("qhgd,khd->hgqk", rows, key_piece, preferred_element_type=jnp.float32) * scale
    )
    key_position = jnp.arange(key_piece.shape[0], dtype=jnp.int32)
    valid = key_position[None, :] <= position[:, None]
    scores = jnp.where(valid, scores, -1e30)
    new_max = jnp.maximum(running_max, jnp.max(scores, axis=-1))
    weights = jnp.where(valid, jnp.exp(scores - new_max[..., None]), 0.0)
    running_sum = jnp.sum(weights, axis=-1)
    update = jnp.einsum(
        "hgqk,khd->hgqd",
        weights.astype(jnp.bfloat16),
        value_piece,
        preferred_element_type=jnp.float32,
    )
    weighted = update
    return (new_max, running_sum, weighted)


def finish(state, half_rows, query_heads, head_size):
    running_max, running_sum, weighted = state
    result = weighted / running_sum[..., None]
    result = jnp.transpose(result, (2, 0, 1, 3)).reshape(half_rows, query_heads, head_size)
    return result.astype(jnp.bfloat16)


def per_device(queries, keys, values):
    local_rows, query_heads, head_size = queries.shape
    key_heads = keys.shape[1]
    group_size = query_heads // key_heads
    half_rows = local_rows // 2
    scale = head_size ** (-0.5)
    context_size = lax.axis_size("ctx")
    position_index = lax.axis_index("ctx")
    offset = jnp.arange(half_rows, dtype=jnp.int32)
    first_rows = queries[:half_rows]
    first_position = position_index * local_rows + offset
    second_rows = queries[half_rows:]
    bit_count = context_size.bit_length() - 1
    for bit_index in range(bit_count):
        second_rows = from_partner(second_rows, "ctx", bit_index)
    second_position = (context_size - 1 - position_index) * local_rows + half_rows + offset
    halves = (
        (first_rows.reshape(half_rows, key_heads, group_size, head_size), first_position),
        (second_rows.reshape(half_rows, key_heads, group_size, head_size), second_position),
    )
    initial = (
        jnp.full((key_heads, group_size, half_rows), -1e30, jnp.float32),
        jnp.zeros((key_heads, group_size, half_rows), jnp.float32),
        jnp.zeros((key_heads, group_size, half_rows, head_size), jnp.float32),
    )
    carries = (initial, initial)
    start = jnp.int32(0)
    key_piece = lax.all_gather(keys, "ctx", axis=0, tiled=True)
    value_piece = lax.all_gather(values, "ctx", axis=0, tiled=True)
    updated = []
    for which in range(2):
        rows, position = halves[which]
        needed = start <= position[-1]
        updated.append(
            lax.cond(
                needed,
                lambda state: attend_piece(state, rows, position, key_piece, value_piece, scale),
                lambda state: state,
                carries[which],
            )
        )
    carries = (updated[0], updated[1])
    first_out = finish(carries[0], half_rows, query_heads, head_size)
    second_out = finish(carries[1], half_rows, query_heads, head_size)
    for bit_index in range(bit_count):
        second_out = from_partner(second_out, "ctx", bit_index)
    return jnp.concatenate([first_out, second_out], axis=0)


def solution(mesh):
    placed = (
        P(("rep", "ctx"), "head", None),
        P(("rep", "ctx"), "head", None),
        P(("rep", "ctx"), "head", None),
    )
    return jax.shard_map(
        per_device,
        mesh=mesh,
        in_specs=placed,
        out_specs=P(("rep", "ctx"), "head", None),
        check_vma=False,
    )
```

profile of v0, /device:TPU:0, one launch (start us, length us, event | category | flops | bytes accessed | tf_op | source)
XLA Modules:
  0.0 91.4 jit_solution(11736791477938292127)
XLA Ops:
  0.0 0.9 slice-done
  0.9 3.0 %collective-permute-start = (bf16[32,16,128]{2,0,1:T(8,128)(2,1)S(1)}, bf16[32,16,128]{2,0,1:T(8,128)(2,1)S(1)}, u32[]{:S(2)}, u32[]{:S(2)}) collective-permute-start(bf16[32,16,128]{2,0,1:T(8,128)(2,1)S(1)} %copy.14), channel_id=1, source_target_pairs={{0,2},{2,0},{4,6},{6,4},{8,10},{10,8},{12,14},{14,12},{1,3},{3,1},... | collective-permute-start | bytes 393224 | tf_op jit(solution)/shard_map/ppermute | solution.py:8
  4.0 3.5 %collective-permute-done = bf16[32,16,128]{2,0,1:T(8,128)(2,1)S(1)} collective-permute-done((bf16[32,16,128]{2,0,1:T(8,128)(2,1)S(1)}, bf16[32,16,128]{2,0,1:T(8,128)(2,1)S(1)}, u32[]{:S(2)}, u32[]{:S(2)}) %collective-permute-start) | collective-permute-done | bytes 131104 | tf_op jit(solution)/shard_map/ppermute | solution.py:8
  7.5 1.8 %collective-permute-start.1 = (bf16[32,16,128]{2,0,1:T(8,128)(2,1)S(1)}, bf16[32,16,128]{2,0,1:T(8,128)(2,1)S(1)}, u32[]{:S(2)}, u32[]{:S(2)}) collective-permute-start(bf16[32,16,128]{2,0,1:T(8,128)(2,1)S(1)} %collective-permute-done), channel_id=1, source_target_pairs={{0,4},{2,6},{4,0},{6,2},{8,12},{10,14},{12,8},{14,10},{1,5},{3,7},... | collective-permute-start | bytes 393224 | tf_op jit(solution)/shard_map/ppermute | solution.py:8
  9.3 31.0 %all_gather.6 = bf16[512,2,128]{2,0,1:T(8,128)(2,1)S(1)} all-gather(bf16[64,2,128]{2,0,1:T(8,128)(2,1)S(1)} %copy.4), channel_id=1, replica_groups=mesh['rep'=2,'ctx'=8,'head'=2] {'ctx'}, dimensions={0}, use_global_device_ids=true | all-gather | bytes 294912 | tf_op jit(solution)/shard_map/all_gather | solution.py:66
  40.4 0.6 slice.14
  41.6 31.0 %all_gather.7 = bf16[512,2,128]{2,0,1:T(8,128)(2,1)S(1)} all-gather(bf16[64,2,128]{2,0,1:T(8,128)(2,1)S(1)} %copy.5), channel_id=1, replica_groups=mesh['rep'=2,'ctx'=8,'head'=2] {'ctx'}, dimensions={0}, use_global_device_ids=true | all-gather | bytes 294912 | tf_op jit(solution)/shard_map/all_gather | solution.py:67
  72.6 1.2 %conditional.3 = (f32[2,8,32]{2,1,0:T(8,128)S(1)}, f32[2,8,32,128]{3,2,1,0:T(8,128)S(1)}) conditional(s32[]{:T(128)} %bitcast.15, () %tuple.23, (s32[32]{0:T(128)S(1)}, bf16[32,16,128]{2,0,1:T(8,128)(2,1)S(1)}, bf16[512,2,128]{2,0,1:T(8,128)(2,1)S(1)}, bf16[512,2,128]{2,0,1:T(8,128)(2,1)S(1)}) %tuple.24), branch_computations={%region_4.5_spmd, %region_5.8_spmd} | conditional | flops 136592896 | bytes 4141200 | solution.py:73
  72.7 0.4 fusion.27
  73.1 0.4 fusion.16
  73.4 0.3 fusion.15
  73.8 0.1 fusion.25
  74.0 0.8 collective-permute-start.3
  74.8 4.2 %collective-permute-done.3 = bf16[32,16,128]{2,1,0:T(8,128)(2,1)S(1)} collective-permute-done((bf16[32,16,128]{2,1,0:T(8,128)(2,1)S(1)}, bf16[32,16,128]{2,1,0:T(8,128)(2,1)S(1)}, u32[]{:S(2)}, u32[]{:S(2)}) %collective-permute-start.3) | collective-permute-done | bytes 131104 | tf_op jit(solution)/shard_map/ppermute | solution.py:8
  79.0 0.6 slice.13
  80.3 1.3 %conditional.2 = (f32[2,8,32]{2,1,0:T(8,128)S(1)}, f32[2,8,32,128]{3,2,1,0:T(8,128)S(1)}) conditional(s32[]{:T(128)} %bitcast.12, () %tuple.21, (s32[32]{0:T(128)S(1)}, bf16[64,16,128]{2,1,0:T(8,128)(2,1)S(1)}, bf16[512,2,128]{2,0,1:T(8,128)(2,1)S(1)}, bf16[512,2,128]{2,0,1:T(8,128)(2,1)S(1)}) %tuple.32), branch_computations={%region_0.0_spmd, %region_1.4_spmd} | conditional | flops 136592896 | bytes 4927632 | solution.py:73
  80.5 0.4 fusion.26
  80.9 0.4 fusion.4
  81.2 0.3 fusion.3
  81.6 2.4 %collective-permute-done.4 = bf16[32,16,128]{2,1,0:T(8,128)(2,1)S(1)} collective-permute-done((bf16[32,16,128]{2,1,0:T(8,128)(2,1)S(1)}, bf16[32,16,128]{2,1,0:T(8,128)(2,1)S(1)}, u32[]{:S(2)}, u32[]{:S(2)}) %collective-permute-start.4) | collective-permute-done | bytes 131104 | tf_op jit(solution)/shard_map/ppermute | solution.py:8
  84.0 0.7 collective-permute-start.5
  84.7 0.1 fusion.24
  84.9 5.8 %collective-permute-done.5 = bf16[32,16,128]{2,1,0:T(8,128)(2,1)S(1)} collective-permute-done((bf16[32,16,128]{2,1,0:T(8,128)(2,1)S(1)}, bf16[32,16,128]{2,1,0:T(8,128)(2,1)S(1)}, u32[]{:S(2)}, u32[]{:S(2)}) %collective-permute-start.5) | collective-permute-done | bytes 131104 | tf_op jit(solution)/shard_map/ppermute | solution.py:8
  90.7 0.7 pad_maximum_fusion
  (24 shorter events, 0.4 us)
Async XLA Ops:
  0.0 0.9 slice-start
  0.9 8.4 %copy-start.1 = (bf16[64,2,128]{2,1,0:T(2,128)(2,1)S(1)}, bf16[64,2,128]{2,1,0:T(2,128)(2,1)}, u32[]{:S(2)}) copy-start(bf16[64,2,128]{2,1,0:T(2,128)(2,1)} %param.8) | copy-start | bytes 98308
  0.9 6.5 %collective-permute-start = (bf16[32,16,128]{2,0,1:T(8,128)(2,1)S(1)}, bf16[32,16,128]{2,0,1:T(8,128)(2,1)S(1)}, u32[]{:S(2)}, u32[]{:S(2)}) collective-permute-start(bf16[32,16,128]{2,0,1:T(8,128)(2,1)S(1)} %copy.14), channel_id=1, source_target_pairs={{0,2},{2,0},{4,6},{6,4},{8,10},{10,8},{12,14},{14,12},{1,3},{3,1},... | collective-permute-start | bytes 393224 | tf_op jit(solution)/shard_map/ppermute | solution.py:8
  7.5 32.9 %collective-permute-start.1 = (bf16[32,16,128]{2,0,1:T(8,128)(2,1)S(1)}, bf16[32,16,128]{2,0,1:T(8,128)(2,1)S(1)}, u32[]{:S(2)}, u32[]{:S(2)}) collective-permute-start(bf16[32,16,128]{2,0,1:T(8,128)(2,1)S(1)} %collective-permute-done), channel_id=1, source_target_pairs={{0,4},{2,6},{4,0},{6,2},{8,12},{10,14},{12,8},{14,10},{1,5},{3,7},... | collective-permute-start | bytes 393224 | tf_op jit(solution)/shard_map/ppermute | solution.py:8
  9.3 31.0 %copy-start.2 = (bf16[64,2,128]{2,1,0:T(2,128)(2,1)S(1)}, bf16[64,2,128]{2,1,0:T(2,128)(2,1)}, u32[]{:S(2)}) copy-start(bf16[64,2,128]{2,1,0:T(2,128)(2,1)} %param.9) | copy-start | bytes 98308
  40.4 32.2 %collective-permute-start.2 = (bf16[32,16,128]{2,0,1:T(8,128)(2,1)S(1)}, bf16[32,16,128]{2,0,1:T(8,128)(2,1)S(1)}, u32[]{:S(2)}, u32[]{:S(2)}) collective-permute-start(bf16[32,16,128]{2,0,1:T(8,128)(2,1)S(1)} %collective-permute-done.1), channel_id=1, source_target_pairs={{0,8},{2,10},{4,12},{6,14},{8,0},{10,2},{12,4},{14,6},{1,9},{3,11}... | collective-permute-start | bytes 393224 | tf_op jit(solution)/shard_map/ppermute | solution.py:8
  73.8 6.5 %copy-start = (bf16[64,16,128]{2,1,0:T(8,128)(2,1)S(1)}, bf16[64,16,128]{2,1,0:T(8,128)(2,1)}, u32[]{:S(2)}) copy-start(bf16[64,16,128]{2,1,0:T(8,128)(2,1)} %param.7) | copy-start | bytes 786436
  74.0 5.0 %collective-permute-start.3 = (bf16[32,16,128]{2,1,0:T(8,128)(2,1)S(1)}, bf16[32,16,128]{2,1,0:T(8,128)(2,1)S(1)}, u32[]{:S(2)}, u32[]{:S(2)}) collective-permute-start(bf16[32,16,128]{2,1,0:T(8,128)(2,1)S(1)} %bitcast.51), channel_id=1, source_target_pairs={{0,2},{2,0},{4,6},{6,4},{8,10},{10,8},{12,14},{14,12},{1,3},{3,1},... | collective-permute-start | bytes 393224 | tf_op jit(solution)/shard_map/ppermute | solution.py:8
  79.0 5.0 %collective-permute-start.4 = (bf16[32,16,128]{2,1,0:T(8,128)(2,1)S(1)}, bf16[32,16,128]{2,1,0:T(8,128)(2,1)S(1)}, u32[]{:S(2)}, u32[]{:S(2)}) collective-permute-start(bf16[32,16,128]{2,1,0:T(8,128)(2,1)S(1)} %collective-permute-done.3), channel_id=1, source_target_pairs={{0,4},{2,6},{4,0},{6,2},{8,12},{10,14},{12,8},{14,10},{1,5},{3,7},... | collective-permute-start | bytes 393224 | tf_op jit(solution)/shard_map/ppermute | solution.py:8
  84.0 6.7 %collective-permute-start.5 = (bf16[32,16,128]{2,1,0:T(8,128)(2,1)S(1)}, bf16[32,16,128]{2,1,0:T(8,128)(2,1)S(1)}, u32[]{:S(2)}, u32[]{:S(2)}) collective-permute-start(bf16[32,16,128]{2,1,0:T(8,128)(2,1)S(1)} %collective-permute-done.4), channel_id=1, source_target_pairs={{0,8},{2,10},{4,12},{6,14},{8,0},{10,2},{12,4},{14,6},{1,9},{3,11}... | collective-permute-start | bytes 393224 | tf_op jit(solution)/shard_map/ppermute | solution.py:8
where the time goes:
time: 91.6 us; the launch traced here: 91.4 us
  blocking collectives  62 us (68%)
  waiting for transfers between devices  15.9 us (17%)
  starting transfers between devices  6.41 us (7%)
  local copies, waits for them, and re-layouts  2.32 us (3%)
  other arithmetic  1.85 us (2%)
  matrix products  1.47 us (2%)
  between operations  1.41 us (2%)
    all_gather x1, blocking collectives, per_device(): key_piece = lax.all_gather(keys, 'ctx', axis=0, tiled=True)  31 us
    all_gather x1, blocking collectives, per_device(): value_piece = lax.all_gather(values, 'ctx', axis=0, tiled=True)  31 us
    ppermute x6, waiting for transfers between devices, from_partner(): lax.ppermute(x, axis, [(i, i ^ 1 << bit) for i in range(lax.axis_size(axi...  15.9 us
    ppermute x6, starting transfers between devices, from_partner(): lax.ppermute(x, axis, [(i, i ^ 1 << bit) for i in range(lax.axis_size(axi...  6.41 us
  transfers between devices with their start and end apart: 6, of which 4 were waited for; matrix products, arithmetic and copies ran while one was open for 3% of the time, Pallas kernels for 0%

commit v1 on v0

v1 whole, which is shorter than its diff:
```python
import jax
import jax.numpy as jnp
from jax import lax
from jax.sharding import PartitionSpec as P


def per_device(queries, keys, values):
    local_rows, query_heads, head_size = queries.shape
    key_heads = keys.shape[1]
    group_size = query_heads // key_heads
    scale = head_size ** (-0.5)
    context_size = lax.axis_size("ctx")
    me = lax.axis_index("ctx")
    offset = jnp.arange(local_rows, dtype=jnp.int32)
    position = me * local_rows + offset
    pair = jnp.concatenate([keys, values], axis=1)
    pieces = [pair]
    sources = [me * local_rows + offset]
    for shift in range(1, context_size):
        pieces.append(lax.ppermute(pair, "ctx", [(i, (i + shift) % context_size) for i in range(context_size)]))
        source = me - shift
        sources.append((source % context_size) * local_rows + offset)
    gathered = jnp.concatenate(pieces, axis=0)
    key_position = jnp.concatenate(sources, axis=0)
    key_all = gathered[:, :key_heads]
    value_all = gathered[:, key_heads:]
    rows = queries.reshape(local_rows, key_heads, group_size, head_size)
    scores = jnp.einsum("qhgd,khd->hgqk", rows, key_all, preferred_element_type=jnp.float32) * scale
    valid = key_position[None, :] <= position[:, None]
    scores = jnp.where(valid, scores, -1e30)
    row_max = jnp.max(scores, axis=-1)
    weights = jnp.where(valid, jnp.exp(scores - row_max[..., None]), 0.0)
    total = jnp.sum(weights, axis=-1)
    summed = jnp.einsum("hgqk,khd->hgqd", weights.astype(jnp.bfloat16), value_all,
                        preferred_element_type=jnp.float32)
    result = summed / total[..., None]
    result = jnp.transpose(result, (2, 0, 1, 3)).reshape(local_rows, query_heads, head_size)
    return result.astype(jnp.bfloat16)


def solution(mesh):
    placed = P(("rep", "ctx"), "head", None)
    return jax.shard_map(per_device, mesh=mesh, in_specs=(placed, placed, placed),
                         out_specs=placed, check_vma=False)
```

time: 91.6 us -> 21.7 us (0.24)
  blocking collectives: 62 us -> 0 us
  waiting for transfers between devices: 15.9 us -> 2.77 us
  starting transfers between devices: 6.41 us -> 13.9 us
  other arithmetic: 1.85 us -> 0.11 us
  between operations: 1.41 us -> 0.09 us
    all_gather x2 -> x0, blocking collectives: 62 us -> none  [the longest x1 31 us: per_device(): key_piece = lax.all_gather(keys, 'ctx', axis=0, tiled=True)]
    ppermute x6 -> x7, waiting for transfers between devices: 15.9 us -> 2.77 us  [per_device(): lax.ppermute(pair, 'ctx', [(i, (i + shift) % context_size) for i in range...]
    ppermute x6 -> x7, starting transfers between devices: 6.41 us -> 13.9 us  [per_device(): lax.ppermute(pair, 'ctx', [(i, (i + shift) % context_size) for i in range...]
    slice x5 -> x0, local copies, waits for them, and re-layouts: 2.08 us -> none  [the longest x2 1.17 us: per_device(): needed = start <= position[-1]]
    sub x0 -> x1, matrix products: none -> 0.96 us  [per_device(): weights = jnp.where(valid, jnp.exp(scores - row_max[..., None]), 0.0)]
  transfers between devices with their start and end apart: 6 -> 7, of which waited for: 4 -> 4; matrix products, arithmetic and copies ran while one was open for 3% -> 1% of each run, Pallas kernels for 0% -> 0%
where the time goes in v1:
time: 21.7 us; the launch traced here: 21.5 us
  starting transfers between devices  13.9 us (64%)
  waiting for transfers between devices  2.77 us (13%)
  local copies, waits for them, and re-layouts  2.65 us (12%)
  matrix products  1.96 us (9%)
    ppermute x7, starting transfers between devices, per_device(): lax.ppermute(pair, 'ctx', [(i, (i + shift) % context_size) for i in range...  13.9 us
    ppermute x7, waiting for transfers between devices, per_device(): lax.ppermute(pair, 'ctx', [(i, (i + shift) % context_size) for i in range...  2.77 us
    dot_general x1, matrix products, per_device(): jnp.einsum('hgqk,khd->hgqd', weights.astype(jnp.bfloat16), value_all, pre...  1 us
    sub x1, matrix products, per_device(): weights = jnp.where(valid, jnp.exp(scores - row_max[..., None]), 0.0)  0.96 us
    unnamed x9, local copies, waits for them, and re-layouts  0.89 us
    convert_element_type x1, local copies, waits for them, and re-layouts, per_device(): return result.astype(jnp.bfloat16)  0.88 us
    concatenate x1, local copies, waits for them, and re-layouts, per_device(): pair = jnp.concatenate([keys, values], axis=1)  0.78 us
  transfers between devices with their start and end apart: 7, of which 4 were waited for; matrix products, arithmetic and copies ran while one was open for 1% of the time, Pallas kernels for 0%

profile of v1, /device:TPU:0, one launch (start us, length us, event | category | flops | bytes accessed | tf_op | source)
XLA Modules:
  0.0 21.5 jit_solution(17678443605334648968)
XLA Ops:
  0.0 0.0 copy-start
  0.0 0.8 %copy_dynamic-update-slice_fusion.3 = (bf16[64,4,128]{2,0,1:T(8,128)(2,1)S(1)}, bf16[512,4,128]{2,0,1:T(8,128)(2,1)S(1)}) fusion(bf16[64,2,128]{2,1,0:T(2,128)(2,1)} %param.4), kind=kLoop, calls=%fused_computation.19 | loop fusion | bytes 98304
  0.8 0.8 %copy_dynamic-update-slice_fusion.1 = (bf16[64,4,128]{2,0,1:T(8,128)(2,1)S(1)}, bf16[512,4,128]{2,0,1:T(8,128)(2,1)S(1)}) fusion(bf16[64,4,128]{2,0,1:T(8,128)(2,1)S(1)} %get-tuple-element.7, bf16[64,2,128]{2,1,0:T(2,128)(2,1)} %param.5, bf16[512,4,128]{2,0,1:T(8,128)(2,1)S(1)} %get-tuple-element.8), kind=kLoop, calls=%fused_computation.17 | loop fusion | bytes 98304 | tf_op jit(solution)/shard_map/concatenate | solution.py:16
  1.6 3.0 %collective-permute-start = (bf16[64,4,128]{2,0,1:T(8,128)(2,1)S(1)}, bf16[64,4,128]{2,0,1:T(8,128)(2,1)S(1)}, u32[]{:S(2)}, u32[]{:S(2)}) collective-permute-start(bf16[64,4,128]{2,0,1:T(8,128)(2,1)S(1)} %get-tuple-element.5), channel_id=1, source_target_pairs={{0,2},{2,4},{4,6},{6,8},{8,10},{10,12},{12,14},{14,0},{1,3},{3,5},... | collective-permute-start | bytes 196616 | tf_op jit(solution)/shard_map/ppermute | solution.py:20
  4.6 1.6 %collective-permute-start.1 = (bf16[64,4,128]{2,0,1:T(8,128)(2,1)S(1)}, bf16[64,4,128]{2,0,1:T(8,128)(2,1)S(1)}, u32[]{:S(2)}, u32[]{:S(2)}) collective-permute-start(bf16[64,4,128]{2,0,1:T(8,128)(2,1)S(1)} %get-tuple-element.5), channel_id=1, source_target_pairs={{0,4},{2,6},{4,8},{6,10},{8,12},{10,14},{12,0},{14,2},{1,5},{3,7},... | collective-permute-start | bytes 196616 | tf_op jit(solution)/shard_map/ppermute | solution.py:20
  6.2 2.6 %collective-permute-start.2 = (bf16[64,4,128]{2,0,1:T(8,128)(2,1)S(1)}, bf16[64,4,128]{2,0,1:T(8,128)(2,1)S(1)}, u32[]{:S(2)}, u32[]{:S(2)}) collective-permute-start(bf16[64,4,128]{2,0,1:T(8,128)(2,1)S(1)} %get-tuple-element.5), channel_id=1, source_target_pairs={{0,6},{2,8},{4,10},{6,12},{8,14},{10,0},{12,2},{14,4},{1,7},{3,9},... | collective-permute-start | bytes 196616 | tf_op jit(solution)/shard_map/ppermute | solution.py:20
  8.8 1.2 %collective-permute-start.3 = (bf16[64,4,128]{2,0,1:T(8,128)(2,1)S(1)}, bf16[64,4,128]{2,0,1:T(8,128)(2,1)S(1)}, u32[]{:S(2)}, u32[]{:S(2)}) collective-permute-start(bf16[64,4,128]{2,0,1:T(8,128)(2,1)S(1)} %get-tuple-element.5), channel_id=1, source_target_pairs={{0,8},{2,10},{4,12},{6,14},{8,0},{10,2},{12,4},{14,6},{1,9},{3,11}... | collective-permute-start | bytes 196616 | tf_op jit(solution)/shard_map/ppermute | solution.py:20
  10.0 2.6 %collective-permute-start.4 = (bf16[64,4,128]{2,0,1:T(8,128)(2,1)S(1)}, bf16[64,4,128]{2,0,1:T(8,128)(2,1)S(1)}, u32[]{:S(2)}, u32[]{:S(2)}) collective-permute-start(bf16[64,4,128]{2,0,1:T(8,128)(2,1)S(1)} %get-tuple-element.5), channel_id=1, source_target_pairs={{0,10},{2,12},{4,14},{6,0},{8,2},{10,4},{12,6},{14,8},{1,11},{3,13... | collective-permute-start | bytes 196616 | tf_op jit(solution)/shard_map/ppermute | solution.py:20
  12.7 0.1 concatenate.9
  12.7 0.1 broadcast_compare_fusion
  12.8 0.0 collective-permute-done
  12.8 1.4 %collective-permute-start.5 = (bf16[64,4,128]{2,0,1:T(8,128)(2,1)S(1)}, bf16[64,4,128]{2,0,1:T(8,128)(2,1)S(1)}, u32[]{:S(2)}, u32[]{:S(2)}) collective-permute-start(bf16[64,4,128]{2,0,1:T(8,128)(2,1)S(1)} %get-tuple-element.5), channel_id=1, source_target_pairs={{0,12},{2,14},{4,0},{6,2},{8,4},{10,6},{12,8},{14,10},{1,13},{3,15... | collective-permute-start | bytes 196616 | tf_op jit(solution)/shard_map/ppermute | solution.py:20
  14.3 0.0 collective-permute-done.1
  14.3 1.5 %collective-permute-start.6 = (bf16[64,4,128]{2,0,1:T(8,128)(2,1)S(1)}, bf16[64,4,128]{2,0,1:T(8,128)(2,1)S(1)}, u32[]{:S(2)}, u32[]{:S(2)}) collective-permute-start(bf16[64,4,128]{2,0,1:T(8,128)(2,1)S(1)} %get-tuple-element.5), channel_id=1, source_target_pairs={{0,14},{2,0},{4,2},{6,4},{8,6},{10,8},{12,10},{14,12},{1,15},{3,1}... | collective-permute-start | bytes 196616 | tf_op jit(solution)/shard_map/ppermute | solution.py:20
  15.8 0.1 collective-permute-done.2
  15.9 0.7 %collective-permute-done.3 = bf16[64,4,128]{2,0,1:T(8,128)(2,1)S(1)} collective-permute-done((bf16[64,4,128]{2,0,1:T(8,128)(2,1)S(1)}, bf16[64,4,128]{2,0,1:T(8,128)(2,1)S(1)}, u32[]{:S(2)}, u32[]{:S(2)}) %collective-permute-start.3) | collective-permute-done | bytes 65568 | tf_op jit(solution)/shard_map/ppermute | solution.py:20
  16.6 0.9 %collective-permute-done.4 = bf16[64,4,128]{2,0,1:T(8,128)(2,1)S(1)} collective-permute-done((bf16[64,4,128]{2,0,1:T(8,128)(2,1)S(1)}, bf16[64,4,128]{2,0,1:T(8,128)(2,1)S(1)}, u32[]{:S(2)}, u32[]{:S(2)}) %collective-permute-start.4) | collective-permute-done | bytes 65568 | tf_op jit(solution)/shard_map/ppermute | solution.py:20
  17.5 1.1 %collective-permute-done.5 = bf16[64,4,128]{2,0,1:T(8,128)(2,1)S(1)} collective-permute-done((bf16[64,4,128]{2,0,1:T(8,128)(2,1)S(1)}, bf16[64,4,128]{2,0,1:T(8,128)(2,1)S(1)}, u32[]{:S(2)}, u32[]{:S(2)}) %collective-permute-start.5) | collective-permute-done | bytes 65568 | tf_op jit(solution)/shard_map/ppermute | solution.py:20
  18.6 0.0 collective-permute-done.6
  18.6 0.0 copy-done
  18.6 1.0 %fusion.28 = f32[2,8,64]{2,1,0:T(8,128)S(1)} fusion(pred[64,512]{1,0:T(8,128)(4,1)S(1)} %broadcast_compare_fusion, bf16[64,2,8,128]{3,2,1,0:T(8,128)(2,1)S(1)} %bitcast.43, bf16[512,4,128]{2,0,1:T(8,128)(2,1)S(1)} %constant_dynamic-update-slice_fusion), kind=kOutput, calls=%fused_computation.41 | convolution fusion | flops 136839680 | bytes 593920 | tf_op jit(solution)/shard_map/sub | solution.py:32
  19.6 1.0 %fusion.3 = bf16[64,2,8,128]{3,0,2,1:T(8,128)(2,1)S(1)} fusion(bf16[512,4,128]{2,0,1:T(8,128)(2,1)S(1)} %constant_dynamic-update-slice_fusion, f32[64,2,8]{0,2,1:T(8,128)S(1)} %bitcast.45, pred[64,512]{1,0:T(8,128)(4,1)S(1)} %broadcast_compare_fusion, bf16[64,2,8,128]{3,2,1,0:T(8,128)(2,1)S(1)} %bitcast.42), kind=kOutput, calls=%fused_computation.6 | convolution fusion | flops 271320576 | bytes 1122304 | tf_op jit(solution)/shard_map/hgqk,khd->hgqd/dot_general | solution.py:34
  20.6 0.9 %copy.7 = bf16[64,16,128]{2,1,0:T(8,128)(2,1)} copy(bf16[64,16,128]{2,0,1:T(8,128)(2,1)S(1)} %bitcast.44) | data formatting | bytes 524288 | tf_op jit(solution)/shard_map/convert_element_type | solution.py:38
  (12 shorter events, 0.1 us)
Async XLA Ops:
  0.0 18.6 %copy-start = (bf16[64,16,128]{2,1,0:T(8,128)(2,1)S(1)}, bf16[64,16,128]{2,1,0:T(8,128)(2,1)}, u32[]{:S(2)}) copy-start(bf16[64,16,128]{2,1,0:T(8,128)(2,1)} %param.3) | copy-start | bytes 786436
  1.6 11.2 %collective-permute-start = (bf16[64,4,128]{2,0,1:T(8,128)(2,1)S(1)}, bf16[64,4,128]{2,0,1:T(8,128)(2,1)S(1)}, u32[]{:S(2)}, u32[]{:S(2)}) collective-permute-start(bf16[64,4,128]{2,0,1:T(8,128)(2,1)S(1)} %get-tuple-element.5), channel_id=1, source_target_pairs={{0,2},{2,4},{4,6},{6,8},{8,10},{10,12},{12,14},{14,0},{1,3},{3,5},... | collective-permute-start | bytes 196616 | tf_op jit(solution)/shard_map/ppermute | solution.py:20
  4.6 9.6 %collective-permute-start.1 = (bf16[64,4,128]{2,0,1:T(8,128)(2,1)S(1)}, bf16[64,4,128]{2,0,1:T(8,128)(2,1)S(1)}, u32[]{:S(2)}, u32[]{:S(2)}) collective-permute-start(bf16[64,4,128]{2,0,1:T(8,128)(2,1)S(1)} %get-tuple-element.5), channel_id=1, source_target_pairs={{0,4},{2,6},{4,8},{6,10},{8,12},{10,14},{12,0},{14,2},{1,5},{3,7},... | collective-permute-start | bytes 196616 | tf_op jit(solution)/shard_map/ppermute | solution.py:20
  6.2 9.7 %collective-permute-start.2 = (bf16[64,4,128]{2,0,1:T(8,128)(2,1)S(1)}, bf16[64,4,128]{2,0,1:T(8,128)(2,1)S(1)}, u32[]{:S(2)}, u32[]{:S(2)}) collective-permute-start(bf16[64,4,128]{2,0,1:T(8,128)(2,1)S(1)} %get-tuple-element.5), channel_id=1, source_target_pairs={{0,6},{2,8},{4,10},{6,12},{8,14},{10,0},{12,2},{14,4},{1,7},{3,9},... | collective-permute-start | bytes 196616 | tf_op jit(solution)/shard_map/ppermute | solution.py:20
  8.8 7.8 %collective-permute-start.3 = (bf16[64,4,128]{2,0,1:T(8,128)(2,1)S(1)}, bf16[64,4,128]{2,0,1:T(8,128)(2,1)S(1)}, u32[]{:S(2)}, u32[]{:S(2)}) collective-permute-start(bf16[64,4,128]{2,0,1:T(8,128)(2,1)S(1)} %get-tuple-element.5), channel_id=1, source_target_pairs={{0,8},{2,10},{4,12},{6,14},{8,0},{10,2},{12,4},{14,6},{1,9},{3,11}... | collective-permute-start | bytes 196616 | tf_op jit(solution)/shard_map/ppermute | solution.py:20
  10.0 7.5 %collective-permute-start.4 = (bf16[64,4,128]{2,0,1:T(8,128)(2,1)S(1)}, bf16[64,4,128]{2,0,1:T(8,128)(2,1)S(1)}, u32[]{:S(2)}, u32[]{:S(2)}) collective-permute-start(bf16[64,4,128]{2,0,1:T(8,128)(2,1)S(1)} %get-tuple-element.5), channel_id=1, source_target_pairs={{0,10},{2,12},{4,14},{6,0},{8,2},{10,4},{12,6},{14,8},{1,11},{3,13... | collective-permute-start | bytes 196616 | tf_op jit(solution)/shard_map/ppermute | solution.py:20
  12.8 5.7 %collective-permute-start.5 = (bf16[64,4,128]{2,0,1:T(8,128)(2,1)S(1)}, bf16[64,4,128]{2,0,1:T(8,128)(2,1)S(1)}, u32[]{:S(2)}, u32[]{:S(2)}) collective-permute-start(bf16[64,4,128]{2,0,1:T(8,128)(2,1)S(1)} %get-tuple-element.5), channel_id=1, source_target_pairs={{0,12},{2,14},{4,0},{6,2},{8,4},{10,6},{12,8},{14,10},{1,13},{3,15... | collective-permute-start | bytes 196616 | tf_op jit(solution)/shard_map/ppermute | solution.py:20
  14.3 4.3 %collective-permute-start.6 = (bf16[64,4,128]{2,0,1:T(8,128)(2,1)S(1)}, bf16[64,4,128]{2,0,1:T(8,128)(2,1)S(1)}, u32[]{:S(2)}, u32[]{:S(2)}) collective-permute-start(bf16[64,4,128]{2,0,1:T(8,128)(2,1)S(1)} %get-tuple-element.5), channel_id=1, source_target_pairs={{0,14},{2,0},{4,2},{6,4},{8,6},{10,8},{12,10},{14,12},{1,15},{3,1}... | collective-permute-start | bytes 196616 | tf_op jit(solution)/shard_map/ppermute | solution.py:20

commit v2 on v1

--- a/solution.py
+++ b/solution.py
@@ -13,17 +13,17 @@
     me = lax.axis_index("ctx")
     offset = jnp.arange(local_rows, dtype=jnp.int32)
     position = me * local_rows + offset
-    pair = jnp.concatenate([keys, values], axis=1)
+    pair = jnp.stack([keys, values], axis=0)
     pieces = [pair]
     sources = [me * local_rows + offset]
     for shift in range(1, context_size):
         pieces.append(lax.ppermute(pair, "ctx", [(i, (i + shift) % context_size) for i in range(context_size)]))
         source = me - shift
         sources.append((source % context_size) * local_rows + offset)
-    gathered = jnp.concatenate(pieces, axis=0)
+    gathered = jnp.concatenate(pieces, axis=1)
     key_position = jnp.concatenate(sources, axis=0)
-    key_all = gathered[:, :key_heads]
-    value_all = gathered[:, key_heads:]
+    key_all = gathered[0]
+    value_all = gathered[1]
     rows = queries.reshape(local_rows, key_heads, group_size, head_size)
     scores = jnp.einsum("qhgd,khd->hgqk", rows, key_all, preferred_element_type=jnp.float32) * scale
     valid = key_position[None, :] <= position[:, None]

time: 21.7 us -> 20.9 us (0.963)
  local copies, waits for them, and re-layouts: 2.65 us -> 1.88 us
    another operation x0 -> x1, local copies, waits for them, and re-layouts: none -> 0.83 us  [per_device(): pair = jnp.stack([keys, values], axis=0)]
    unnamed x9 -> x8, local copies, waits for them, and re-layouts: 0.89 us -> 0.08 us
    concatenate x2 -> x1, local copies, waits for them, and re-layouts: 0.8 us -> 0.01 us  [per_device(): gathered = jnp.concatenate(pieces, axis=1)]
where the time goes in v2:
time: 20.9 us; the launch traced here: 20.7 us
  starting transfers between devices  13.9 us (67%)
  waiting for transfers between devices  2.77 us (13%)
  matrix products  1.95 us (9%)
  local copies, waits for them, and re-layouts  1.88 us (9%)
    ppermute x7, starting transfers between devices, per_device(): lax.ppermute(pair, 'ctx', [(i, (i + shift) % context_size) for i in range...  13.9 us
    ppermute x7, waiting for transfers between devices, per_device(): lax.ppermute(pair, 'ctx', [(i, (i + shift) % context_size) for i in range...  2.77 us
    dot_general x1, matrix products, per_device(): jnp.einsum('hgqk,khd->hgqd', weights.astype(jnp.bfloat16), value_all, pre...  0.99 us
    sub x1, matrix products, per_device(): weights = jnp.where(valid, jnp.exp(scores - row_max[..., None]), 0.0)  0.96 us
    convert_element_type x1, local copies, waits for them, and re-layouts, per_device(): return result.astype(jnp.bfloat16)  0.88 us
    another operation x1, local copies, waits for them, and re-layouts, per_device(): pair = jnp.stack([keys, values], axis=0)  0.83 us
  transfers between devices with their start and end apart: 7, of which 4 were waited for; matrix products, arithmetic and copies ran while one was open for 1% of the time, Pallas kernels for 0%

profile of v2, /device:TPU:0, one launch (start us, length us, event | category | flops | bytes accessed | tf_op | source)
XLA Modules:
  0.0 20.7 jit_solution(9175696684384162702)
XLA Ops:
  0.0 0.0 copy-start
  0.0 0.8 %copy_bitcast_fusion = (bf16[1,64,2,128]{3,1,2,0:T(8,128)(2,1)S(1)}, bf16[1,64,2,128]{3,1,2,0:T(8,128)(2,1)S(1)}) fusion(bf16[64,2,128]{2,1,0:T(2,128)(2,1)} %param.5, bf16[64,2,128]{2,1,0:T(2,128)(2,1)} %param.4), kind=kLoop, calls=%fused_computation.17 | loop fusion | bytes 131072 | tf_op jit(solution)/shard_map/stack | solution.py:16
  0.9 3.0 %collective-permute-start = (bf16[2,64,2,128]{3,1,2,0:T(8,128)(2,1)S(1)}, bf16[2,64,2,128]{3,1,2,0:T(8,128)(2,1)S(1)}, u32[]{:S(2)}, u32[]{:S(2)}) collective-permute-start(bf16[2,64,2,128]{3,1,2,0:T(8,128)(2,1)S(1)} %get-tuple-element.5), channel_id=1, source_target_pairs={{0,2},{2,4},{4,6},{6,8},{8,10},{10,12},{12,14},{14,0},{1,3},{3,5},... | collective-permute-start | bytes 196616 | tf_op jit(solution)/shard_map/ppermute | solution.py:20
  3.9 1.6 %collective-permute-start.1 = (bf16[2,64,2,128]{3,1,2,0:T(8,128)(2,1)S(1)}, bf16[2,64,2,128]{3,1,2,0:T(8,128)(2,1)S(1)}, u32[]{:S(2)}, u32[]{:S(2)}) collective-permute-start(bf16[2,64,2,128]{3,1,2,0:T(8,128)(2,1)S(1)} %get-tuple-element.5), channel_id=1, source_target_pairs={{0,4},{2,6},{4,8},{6,10},{8,12},{10,14},{12,0},{14,2},{1,5},{3,7},... | collective-permute-start | bytes 196616 | tf_op jit(solution)/shard_map/ppermute | solution.py:20
  5.5 2.6 %collective-permute-start.2 = (bf16[2,64,2,128]{3,1,2,0:T(8,128)(2,1)S(1)}, bf16[2,64,2,128]{3,1,2,0:T(8,128)(2,1)S(1)}, u32[]{:S(2)}, u32[]{:S(2)}) collective-permute-start(bf16[2,64,2,128]{3,1,2,0:T(8,128)(2,1)S(1)} %get-tuple-element.5), channel_id=1, source_target_pairs={{0,6},{2,8},{4,10},{6,12},{8,14},{10,0},{12,2},{14,4},{1,7},{3,9},... | collective-permute-start | bytes 196616 | tf_op jit(solution)/shard_map/ppermute | solution.py:20
  8.0 1.2 %collective-permute-start.3 = (bf16[2,64,2,128]{3,1,2,0:T(8,128)(2,1)S(1)}, bf16[2,64,2,128]{3,1,2,0:T(8,128)(2,1)S(1)}, u32[]{:S(2)}, u32[]{:S(2)}) collective-permute-start(bf16[2,64,2,128]{3,1,2,0:T(8,128)(2,1)S(1)} %get-tuple-element.5), channel_id=1, source_target_pairs={{0,8},{2,10},{4,12},{6,14},{8,0},{10,2},{12,4},{14,6},{1,9},{3,11}... | collective-permute-start | bytes 196616 | tf_op jit(solution)/shard_map/ppermute | solution.py:20
  9.3 2.6 %collective-permute-start.4 = (bf16[2,64,2,128]{3,1,2,0:T(8,128)(2,1)S(1)}, bf16[2,64,2,128]{3,1,2,0:T(8,128)(2,1)S(1)}, u32[]{:S(2)}, u32[]{:S(2)}) collective-permute-start(bf16[2,64,2,128]{3,1,2,0:T(8,128)(2,1)S(1)} %get-tuple-element.5), channel_id=1, source_target_pairs={{0,10},{2,12},{4,14},{6,0},{8,2},{10,4},{12,6},{14,8},{1,11},{3,13... | collective-permute-start | bytes 196616 | tf_op jit(solution)/shard_map/ppermute | solution.py:20
  11.9 0.1 concatenate.6
  12.0 0.1 broadcast_compare_fusion
  12.1 0.0 collective-permute-done
  12.1 1.4 %collective-permute-start.5 = (bf16[2,64,2,128]{3,1,2,0:T(8,128)(2,1)S(1)}, bf16[2,64,2,128]{3,1,2,0:T(8,128)(2,1)S(1)}, u32[]{:S(2)}, u32[]{:S(2)}) collective-permute-start(bf16[2,64,2,128]{3,1,2,0:T(8,128)(2,1)S(1)} %get-tuple-element.5), channel_id=1, source_target_pairs={{0,12},{2,14},{4,0},{6,2},{8,4},{10,6},{12,8},{14,10},{1,13},{3,15... | collective-permute-start | bytes 196616 | tf_op jit(solution)/shard_map/ppermute | solution.py:20
  13.5 0.0 collective-permute-done.1
  13.5 1.5 %collective-permute-start.6 = (bf16[2,64,2,128]{3,1,2,0:T(8,128)(2,1)S(1)}, bf16[2,64,2,128]{3,1,2,0:T(8,128)(2,1)S(1)}, u32[]{:S(2)}, u32[]{:S(2)}) collective-permute-start(bf16[2,64,2,128]{3,1,2,0:T(8,128)(2,1)S(1)} %get-tuple-element.5), channel_id=1, source_target_pairs={{0,14},{2,0},{4,2},{6,4},{8,6},{10,8},{12,10},{14,12},{1,15},{3,1}... | collective-permute-start | bytes 196616 | tf_op jit(solution)/shard_map/ppermute | solution.py:20
  15.0 0.1 collective-permute-done.2
  15.2 0.7 %collective-permute-done.3 = bf16[2,64,2,128]{3,1,2,0:T(8,128)(2,1)S(1)} collective-permute-done((bf16[2,64,2,128]{3,1,2,0:T(8,128)(2,1)S(1)}, bf16[2,64,2,128]{3,1,2,0:T(8,128)(2,1)S(1)}, u32[]{:S(2)}, u32[]{:S(2)}) %collective-permute-start.3) | collective-permute-done | bytes 65568 | tf_op jit(solution)/shard_map/ppermute | solution.py:20
  15.9 0.9 %collective-permute-done.4 = bf16[2,64,2,128]{3,1,2,0:T(8,128)(2,1)S(1)} collective-permute-done((bf16[2,64,2,128]{3,1,2,0:T(8,128)(2,1)S(1)}, bf16[2,64,2,128]{3,1,2,0:T(8,128)(2,1)S(1)}, u32[]{:S(2)}, u32[]{:S(2)}) %collective-permute-start.4) | collective-permute-done | bytes 65568 | tf_op jit(solution)/shard_map/ppermute | solution.py:20
  16.8 1.1 %collective-permute-done.5 = bf16[2,64,2,128]{3,1,2,0:T(8,128)(2,1)S(1)} collective-permute-done((bf16[2,64,2,128]{3,1,2,0:T(8,128)(2,1)S(1)}, bf16[2,64,2,128]{3,1,2,0:T(8,128)(2,1)S(1)}, u32[]{:S(2)}, u32[]{:S(2)}) %collective-permute-start.5) | collective-permute-done | bytes 65568 | tf_op jit(solution)/shard_map/ppermute | solution.py:20
  17.8 0.0 collective-permute-done.6
  17.9 0.0 copy-done
  17.9 1.0 %fusion.28 = f32[2,8,64]{2,1,0:T(8,128)S(1)} fusion(pred[64,512]{1,0:T(8,128)(4,1)S(1)} %broadcast_compare_fusion, bf16[64,2,8,128]{3,2,1,0:T(8,128)(2,1)S(1)} %bitcast.49, bf16[2,512,2,128]{3,1,2,0:T(8,128)(2,1)S(1)} %constant_dynamic-update-slice_fusion), kind=kOutput, calls=%fused_computation.41 | convolution fusion | flops 136839680 | bytes 593920 | tf_op jit(solution)/shard_map/sub | solution.py:32
  18.9 1.0 %fusion.3 = bf16[64,2,8,128]{3,0,2,1:T(8,128)(2,1)S(1)} fusion(bf16[2,512,2,128]{3,1,2,0:T(8,128)(2,1)S(1)} %constant_dynamic-update-slice_fusion, f32[64,2,8]{0,2,1:T(8,128)S(1)} %bitcast.51, pred[64,512]{1,0:T(8,128)(4,1)S(1)} %broadcast_compare_fusion, bf16[64,2,8,128]{3,2,1,0:T(8,128)(2,1)S(1)} %bitcast.48), kind=kOutput, calls=%fused_computation.6 | convolution fusion | flops 271320576 | bytes 1122304 | tf_op jit(solution)/shard_map/hgqk,khd->hgqd/dot_general | solution.py:34
  19.9 0.9 %copy.7 = bf16[64,16,128]{2,1,0:T(8,128)(2,1)} copy(bf16[64,16,128]{2,0,1:T(8,128)(2,1)S(1)} %bitcast.50) | data formatting | bytes 524288 | tf_op jit(solution)/shard_map/convert_element_type | solution.py:38
  (13 shorter events, 0.1 us)
Async XLA Ops:
  0.0 17.9 %copy-start = (bf16[64,16,128]{2,1,0:T(8,128)(2,1)S(1)}, bf16[64,16,128]{2,1,0:T(8,128)(2,1)}, u32[]{:S(2)}) copy-start(bf16[64,16,128]{2,1,0:T(8,128)(2,1)} %param.3) | copy-start | bytes 786436
  0.9 11.2 %collective-permute-start = (bf16[2,64,2,128]{3,1,2,0:T(8,128)(2,1)S(1)}, bf16[2,64,2,128]{3,1,2,0:T(8,128)(2,1)S(1)}, u32[]{:S(2)}, u32[]{:S(2)}) collective-permute-start(bf16[2,64,2,128]{3,1,2,0:T(8,128)(2,1)S(1)} %get-tuple-element.5), channel_id=1, source_target_pairs={{0,2},{2,4},{4,6},{6,8},{8,10},{10,12},{12,14},{14,0},{1,3},{3,5},... | collective-permute-start | bytes 196616 | tf_op jit(solution)/shard_map/ppermute | solution.py:20
  3.9 9.6 %collective-permute-start.1 = (bf16[2,64,2,128]{3,1,2,0:T(8,128)(2,1)S(1)}, bf16[2,64,2,128]{3,1,2,0:T(8,128)(2,1)S(1)}, u32[]{:S(2)}, u32[]{:S(2)}) collective-permute-start(bf16[2,64,2,128]{3,1,2,0:T(8,128)(2,1)S(1)} %get-tuple-element.5), channel_id=1, source_target_pairs={{0,4},{2,6},{4,8},{6,10},{8,12},{10,14},{12,0},{14,2},{1,5},{3,7},... | collective-permute-start | bytes 196616 | tf_op jit(solution)/shard_map/ppermute | solution.py:20
  5.5 9.7 %collective-permute-start.2 = (bf16[2,64,2,128]{3,1,2,0:T(8,128)(2,1)S(1)}, bf16[2,64,2,128]{3,1,2,0:T(8,128)(2,1)S(1)}, u32[]{:S(2)}, u32[]{:S(2)}) collective-permute-start(bf16[2,64,2,128]{3,1,2,0:T(8,128)(2,1)S(1)} %get-tuple-element.5), channel_id=1, source_target_pairs={{0,6},{2,8},{4,10},{6,12},{8,14},{10,0},{12,2},{14,4},{1,7},{3,9},... | collective-permute-start | bytes 196616 | tf_op jit(solution)/shard_map/ppermute | solution.py:20
  8.0 7.8 %collective-permute-start.3 = (bf16[2,64,2,128]{3,1,2,0:T(8,128)(2,1)S(1)}, bf16[2,64,2,128]{3,1,2,0:T(8,128)(2,1)S(1)}, u32[]{:S(2)}, u32[]{:S(2)}) collective-permute-start(bf16[2,64,2,128]{3,1,2,0:T(8,128)(2,1)S(1)} %get-tuple-element.5), channel_id=1, source_target_pairs={{0,8},{2,10},{4,12},{6,14},{8,0},{10,2},{12,4},{14,6},{1,9},{3,11}... | collective-permute-start | bytes 196616 | tf_op jit(solution)/shard_map/ppermute | solution.py:20
  9.3 7.5 %collective-permute-start.4 = (bf16[2,64,2,128]{3,1,2,0:T(8,128)(2,1)S(1)}, bf16[2,64,2,128]{3,1,2,0:T(8,128)(2,1)S(1)}, u32[]{:S(2)}, u32[]{:S(2)}) collective-permute-start(bf16[2,64,2,128]{3,1,2,0:T(8,128)(2,1)S(1)} %get-tuple-element.5), channel_id=1, source_target_pairs={{0,10},{2,12},{4,14},{6,0},{8,2},{10,4},{12,6},{14,8},{1,11},{3,13... | collective-permute-start | bytes 196616 | tf_op jit(solution)/shard_map/ppermute | solution.py:20
  12.1 5.7 %collective-permute-start.5 = (bf16[2,64,2,128]{3,1,2,0:T(8,128)(2,1)S(1)}, bf16[2,64,2,128]{3,1,2,0:T(8,128)(2,1)S(1)}, u32[]{:S(2)}, u32[]{:S(2)}) collective-permute-start(bf16[2,64,2,128]{3,1,2,0:T(8,128)(2,1)S(1)} %get-tuple-element.5), channel_id=1, source_target_pairs={{0,12},{2,14},{4,0},{6,2},{8,4},{10,6},{12,8},{14,10},{1,13},{3,15... | collective-permute-start | bytes 196616 | tf_op jit(solution)/shard_map/ppermute | solution.py:20
  13.5 4.3 %collective-permute-start.6 = (bf16[2,64,2,128]{3,1,2,0:T(8,128)(2,1)S(1)}, bf16[2,64,2,128]{3,1,2,0:T(8,128)(2,1)S(1)}, u32[]{:S(2)}, u32[]{:S(2)}) collective-permute-start(bf16[2,64,2,128]{3,1,2,0:T(8,128)(2,1)S(1)} %get-tuple-element.5), channel_id=1, source_target_pairs={{0,14},{2,0},{4,2},{6,4},{8,6},{10,8},{12,10},{14,12},{1,15},{3,1}... | collective-permute-start | bytes 196616 | tf_op jit(solution)/shard_map/ppermute | solution.py:20

commit v3 on v2

--- a/solution.py
+++ b/solution.py
@@ -14,12 +14,16 @@
     offset = jnp.arange(local_rows, dtype=jnp.int32)
     position = me * local_rows + offset
     pair = jnp.stack([keys, values], axis=0)
-    pieces = [pair]
-    sources = [me * local_rows + offset]
+    moved = {}
+    after = {6: 1, 7: 2} if context_size == 8 else {}
     for shift in range(1, context_size):
-        pieces.append(lax.ppermute(pair, "ctx", [(i, (i + shift) % context_size) for i in range(context_size)]))
-        source = me - shift
-        sources.append((source % context_size) * local_rows + offset)
+        operand = pair
+        if shift in after:
+            operand = lax.optimization_barrier((pair, moved[after[shift]]))[0]
+        moved[shift] = lax.ppermute(operand, "ctx", [(i, (i + shift) % context_size) for i in range(context_size)])
+    order = [5, 4, 3, 2, 1, 6, 7] if context_size == 8 else list(range(1, context_size))
+    pieces = [pair] + [moved[shift] for shift in order]
+    sources = [me * local_rows + offset] + [((me - shift) % context_size) * local_rows + offset for shift in order]
     gathered = jnp.concatenate(pieces, axis=1)
     key_position = jnp.concatenate(sources, axis=0)
     key_all = gathered[0]
@@ -29,7 +33,7 @@
     valid = key_position[None, :] <= position[:, None]
     scores = jnp.where(valid, scores, -1e30)
     row_max = jnp.max(scores, axis=-1)
-    weights = jnp.where(valid, jnp.exp(scores - row_max[..., None]), 0.0)
+    weights = jnp.exp(scores - row_max[..., None])
     total = jnp.sum(weights, axis=-1)
     summed = jnp.einsum("hgqk,khd->hgqd", weights.astype(jnp.bfloat16), value_all,
                         preferred_element_type=jnp.float32)

time: 20.9 us -> 20.7 us (level)
  matrix products: 1.95 us -> 1.11 us
  other arithmetic: 0.13 us -> 0.78 us
    sub x1 -> x0, matrix products: 0.96 us -> none  [per_device(): weights = jnp.where(valid, jnp.exp(scores - row_max[..., None]), 0.0)]
    reduce_sum x0 -> x1, other arithmetic: none -> 0.65 us  [per_device(): total = jnp.sum(weights, axis=-1)]
    dot_general x0 -> x1, matrix products: none -> 0.54 us  [per_device(): jnp.einsum('qhgd,khd->hgqk', rows, key_all, preferred_element_type=jnp.fl...]
    dot_general x1, matrix products: 0.99 us -> 0.58 us  [per_device(): jnp.einsum('hgqk,khd->hgqd', weights.astype(jnp.bfloat16), value_all, pre...]
  transfers between devices with their start and end apart: 7 -> 7, of which waited for: 4 -> 2; matrix products, arithmetic and copies ran while one was open for 1% -> 1% of each run, Pallas kernels for 0% -> 0%
where the time goes in v3:
time: 20.7 us; the launch traced here: 20.5 us
  starting transfers between devices  13.8 us (67%)
  waiting for transfers between devices  2.79 us (13%)
  local copies, waits for them, and re-layouts  1.89 us (9%)
  matrix products  1.11 us (5%)
  other arithmetic  0.78 us (4%)
    ppermute x7, starting transfers between devices, per_device(): lax.ppermute(operand, 'ctx', [(i, (i + shift) % context_size) for i in ra...  13.8 us
    ppermute x7, waiting for transfers between devices, per_device(): lax.ppermute(operand, 'ctx', [(i, (i + shift) % context_size) for i in ra...  2.79 us
    convert_element_type x1, local copies, waits for them, and re-layouts, per_device(): return result.astype(jnp.bfloat16)  0.88 us
    another operation x1, local copies, waits for them, and re-layouts, per_device(): pair = jnp.stack([keys, values], axis=0)  0.83 us
    reduce_sum x1, other arithmetic, per_device(): total = jnp.sum(weights, axis=-1)  0.65 us
    dot_general x1, matrix products, per_device(): jnp.einsum('hgqk,khd->hgqd', weights.astype(jnp.bfloat16), value_all, pre...  0.58 us
    dot_general x1, matrix products, per_device(): jnp.einsum('qhgd,khd->hgqk', rows, key_all, preferred_element_type=jnp.fl...  0.54 us
  transfers between devices with their start and end apart: 7, of which 2 were waited for; matrix products, arithmetic and copies ran while one was open for 1% of the time, Pallas kernels for 0%

profile of v3, /device:TPU:0, one launch (start us, length us, event | category | flops | bytes accessed | tf_op | source)
XLA Modules:
  0.0 20.5 jit_solution(2874911489653572063)
XLA Ops:
  0.0 0.0 copy-start
  0.0 0.8 %copy_bitcast_fusion = (bf16[1,64,2,128]{3,1,2,0:T(8,128)(2,1)S(1)}, bf16[1,64,2,128]{3,1,2,0:T(8,128)(2,1)S(1)}) fusion(bf16[64,2,128]{2,1,0:T(2,128)(2,1)} %param.5, bf16[64,2,128]{2,1,0:T(2,128)(2,1)} %param.4), kind=kLoop, calls=%fused_computation.13 | loop fusion | bytes 131072 | tf_op jit(solution)/shard_map/stack | solution.py:16
  0.9 3.0 %collective-permute-start.4 = (bf16[2,64,2,128]{3,1,2,0:T(8,128)(2,1)S(1)}, bf16[2,64,2,128]{3,1,2,0:T(8,128)(2,1)S(1)}, u32[]{:S(2)}, u32[]{:S(2)}) collective-permute-start(bf16[2,64,2,128]{3,1,2,0:T(8,128)(2,1)S(1)} %get-tuple-element.8), channel_id=1, source_target_pairs={{0,2},{2,4},{4,6},{6,8},{8,10},{10,12},{12,14},{14,0},{1,3},{3,5},... | collective-permute-start | bytes 196616 | tf_op jit(solution)/shard_map/ppermute | solution.py:23
  3.9 1.6 %collective-permute-start.3 = (bf16[2,64,2,128]{3,1,2,0:T(8,128)(2,1)S(1)}, bf16[2,64,2,128]{3,1,2,0:T(8,128)(2,1)S(1)}, u32[]{:S(2)}, u32[]{:S(2)}) collective-permute-start(bf16[2,64,2,128]{3,1,2,0:T(8,128)(2,1)S(1)} %get-tuple-element.8), channel_id=1, source_target_pairs={{0,4},{2,6},{4,8},{6,10},{8,12},{10,14},{12,0},{14,2},{1,5},{3,7},... | collective-permute-start | bytes 196616 | tf_op jit(solution)/shard_map/ppermute | solution.py:23
  5.5 2.6 %collective-permute-start.2 = (bf16[2,64,2,128]{3,1,2,0:T(8,128)(2,1)S(1)}, bf16[2,64,2,128]{3,1,2,0:T(8,128)(2,1)S(1)}, u32[]{:S(2)}, u32[]{:S(2)}) collective-permute-start(bf16[2,64,2,128]{3,1,2,0:T(8,128)(2,1)S(1)} %get-tuple-element.8), channel_id=1, source_target_pairs={{0,6},{2,8},{4,10},{6,12},{8,14},{10,0},{12,2},{14,4},{1,7},{3,9},... | collective-permute-start | bytes 196616 | tf_op jit(solution)/shard_map/ppermute | solution.py:23
  8.0 1.2 %collective-permute-start.1 = (bf16[2,64,2,128]{3,1,2,0:T(8,128)(2,1)S(1)}, bf16[2,64,2,128]{3,1,2,0:T(8,128)(2,1)S(1)}, u32[]{:S(2)}, u32[]{:S(2)}) collective-permute-start(bf16[2,64,2,128]{3,1,2,0:T(8,128)(2,1)S(1)} %get-tuple-element.8), channel_id=1, source_target_pairs={{0,8},{2,10},{4,12},{6,14},{8,0},{10,2},{12,4},{14,6},{1,9},{3,11}... | collective-permute-start | bytes 196616 | tf_op jit(solution)/shard_map/ppermute | solution.py:23
  9.3 2.6 %collective-permute-start = (bf16[2,64,2,128]{3,1,2,0:T(8,128)(2,1)S(1)}, bf16[2,64,2,128]{3,1,2,0:T(8,128)(2,1)S(1)}, u32[]{:S(2)}, u32[]{:S(2)}) collective-permute-start(bf16[2,64,2,128]{3,1,2,0:T(8,128)(2,1)S(1)} %get-tuple-element.8), channel_id=1, source_target_pairs={{0,10},{2,12},{4,14},{6,0},{8,2},{10,4},{12,6},{14,8},{1,11},{3,13... | collective-permute-start | bytes 196616 | tf_op jit(solution)/shard_map/ppermute | solution.py:23
  11.9 0.1 concatenate.6
  12.0 0.1 broadcast_compare_fusion
  12.1 0.0 collective-permute-done.4
  12.1 1.4 %collective-permute-start.5 = (bf16[2,64,2,128]{3,1,2,0:T(8,128)(2,1)S(1)}, bf16[2,64,2,128]{3,1,2,0:T(8,128)(2,1)S(1)}, u32[]{:S(2)}, u32[]{:S(2)}) collective-permute-start(bf16[2,64,2,128]{3,1,2,0:T(8,128)(2,1)S(1)} %get-tuple-element.8), channel_id=1, source_target_pairs={{0,12},{2,14},{4,0},{6,2},{8,4},{10,6},{12,8},{14,10},{1,13},{3,15... | collective-permute-start | bytes 196616 | tf_op jit(solution)/shard_map/ppermute | solution.py:23
  13.5 0.0 collective-permute-done.3
  13.5 1.4 %collective-permute-start.6 = (bf16[2,64,2,128]{3,1,2,0:T(8,128)(2,1)S(1)}, bf16[2,64,2,128]{3,1,2,0:T(8,128)(2,1)S(1)}, u32[]{:S(2)}, u32[]{:S(2)}) collective-permute-start(bf16[2,64,2,128]{3,1,2,0:T(8,128)(2,1)S(1)} %get-tuple-element.8), channel_id=1, source_target_pairs={{0,14},{2,0},{4,2},{6,4},{8,6},{10,8},{12,10},{14,12},{1,15},{3,1}... | collective-permute-start | bytes 196616 | tf_op jit(solution)/shard_map/ppermute | solution.py:23
  14.9 1.8 %collective-permute-done = bf16[2,64,2,128]{3,1,2,0:T(8,128)(2,1)S(1)} collective-permute-done((bf16[2,64,2,128]{3,1,2,0:T(8,128)(2,1)S(1)}, bf16[2,64,2,128]{3,1,2,0:T(8,128)(2,1)S(1)}, u32[]{:S(2)}, u32[]{:S(2)}) %collective-permute-start) | collective-permute-done | bytes 65568 | tf_op jit(solution)/shard_map/ppermute | solution.py:23
  16.8 0.0 collective-permute-done.1
  16.8 0.0 collective-permute-done.2
  16.9 1.0 %collective-permute-done.5 = bf16[2,64,2,128]{3,1,2,0:T(8,128)(2,1)S(1)} collective-permute-done((bf16[2,64,2,128]{3,1,2,0:T(8,128)(2,1)S(1)}, bf16[2,64,2,128]{3,1,2,0:T(8,128)(2,1)S(1)}, u32[]{:S(2)}, u32[]{:S(2)}) %collective-permute-start.5) | collective-permute-done | bytes 65568 | tf_op jit(solution)/shard_map/ppermute | solution.py:23
  17.8 0.0 collective-permute-done.6
  17.9 0.0 copy-done
  17.9 0.5 %fusion.7 = (f32[2,8,64]{2,1,0:T(8,128)S(1)}, f32[2,8,64,512]{3,2,1,0:T(8,128)S(1)}) fusion(bf16[64,2,8,128]{3,2,1,0:T(8,128)(2,1)S(1)} %bitcast.29, bf16[2,512,2,128]{3,1,2,0:T(8,128)(2,1)S(1)} %constant_dynamic-update-slice_fusion, pred[64,512]{1,0:T(8,128)(4,1)S(1)} %broadcast_compare_fusion), kind=kOutput, calls=%fused_computation.31 | convolution fusion | flops 135789568 | bytes 2658304 | tf_op jit(solution)/shard_map/qhgd,khd->hgqk/dot_general | solution.py:32
  18.4 0.6 %fusion = f32[2,8,64]{2,1,0:T(8,128)S(1)} fusion(f32[2,8,64,512]{3,2,1,0:T(8,128)S(1)} %get-tuple-element.12, f32[2,8,64]{2,1,0:T(8,128)S(1)} %get-tuple-element.11), kind=kLoop, calls=%fused_computation.2 | loop fusion | flops 1047552 | bytes 2105344 | tf_op jit(solution)/shard_map/reduce_sum | solution.py:37
  19.1 0.6 %fusion.3 = bf16[64,2,8,128]{3,0,2,1:T(8,128)(2,1)S(1)} fusion(f32[2,8,64,512]{3,2,1,0:T(8,128)S(1)} %get-tuple-element.12, f32[2,8,64]{2,1,0:T(8,128)S(1)} %get-tuple-element.11, bf16[2,512,2,128]{3,1,2,0:T(8,128)(2,1)S(1)} %constant_dynamic-update-slice_fusion, f32[64,2,8]{0,2,1:T(8,128)S(1)} %bitcast.31), kind=kOutput, calls=%fused_computation.6 | convolution fusion | flops 135528448 | bytes 2637824 | tf_op jit(solution)/shard_map/hgqk,khd->hgqd/dot_general | solution.py:38
  19.7 0.9 %copy.7 = bf16[64,16,128]{2,1,0:T(8,128)(2,1)} copy(bf16[64,16,128]{2,0,1:T(8,128)(2,1)S(1)} %bitcast.30) | data formatting | bytes 524288 | tf_op jit(solution)/shard_map/convert_element_type | solution.py:42
  (13 shorter events, 0.1 us)
Async XLA Ops:
  0.0 17.9 %copy-start = (bf16[64,16,128]{2,1,0:T(8,128)(2,1)S(1)}, bf16[64,16,128]{2,1,0:T(8,128)(2,1)}, u32[]{:S(2)}) copy-start(bf16[64,16,128]{2,1,0:T(8,128)(2,1)} %param.3) | copy-start | bytes 786436
  0.9 11.2 %collective-permute-start.4 = (bf16[2,64,2,128]{3,1,2,0:T(8,128)(2,1)S(1)}, bf16[2,64,2,128]{3,1,2,0:T(8,128)(2,1)S(1)}, u32[]{:S(2)}, u32[]{:S(2)}) collective-permute-start(bf16[2,64,2,128]{3,1,2,0:T(8,128)(2,1)S(1)} %get-tuple-element.8), channel_id=1, source_target_pairs={{0,2},{2,4},{4,6},{6,8},{8,10},{10,12},{12,14},{14,0},{1,3},{3,5},... | collective-permute-start | bytes 196616 | tf_op jit(solution)/shard_map/ppermute | solution.py:23
  3.9 9.6 %collective-permute-start.3 = (bf16[2,64,2,128]{3,1,2,0:T(8,128)(2,1)S(1)}, bf16[2,64,2,128]{3,1,2,0:T(8,128)(2,1)S(1)}, u32[]{:S(2)}, u32[]{:S(2)}) collective-permute-start(bf16[2,64,2,128]{3,1,2,0:T(8,128)(2,1)S(1)} %get-tuple-element.8), channel_id=1, source_target_pairs={{0,4},{2,6},{4,8},{6,10},{8,12},{10,14},{12,0},{14,2},{1,5},{3,7},... | collective-permute-start | bytes 196616 | tf_op jit(solution)/shard_map/ppermute | solution.py:23
  5.5 11.3 %collective-permute-start.2 = (bf16[2,64,2,128]{3,1,2,0:T(8,128)(2,1)S(1)}, bf16[2,64,2,128]{3,1,2,0:T(8,128)(2,1)S(1)}, u32[]{:S(2)}, u32[]{:S(2)}) collective-permute-start(bf16[2,64,2,128]{3,1,2,0:T(8,128)(2,1)S(1)} %get-tuple-element.8), channel_id=1, source_target_pairs={{0,6},{2,8},{4,10},{6,12},{8,14},{10,0},{12,2},{14,4},{1,7},{3,9},... | collective-permute-start | bytes 196616 | tf_op jit(solution)/shard_map/ppermute | solution.py:23
  8.0 8.7 %collective-permute-start.1 = (bf16[2,64,2,128]{3,1,2,0:T(8,128)(2,1)S(1)}, bf16[2,64,2,128]{3,1,2,0:T(8,128)(2,1)S(1)}, u32[]{:S(2)}, u32[]{:S(2)}) collective-permute-start(bf16[2,64,2,128]{3,1,2,0:T(8,128)(2,1)S(1)} %get-tuple-element.8), channel_id=1, source_target_pairs={{0,8},{2,10},{4,12},{6,14},{8,0},{10,2},{12,4},{14,6},{1,9},{3,11}... | collective-permute-start | bytes 196616 | tf_op jit(solution)/shard_map/ppermute | solution.py:23
  9.3 7.5 %collective-permute-start = (bf16[2,64,2,128]{3,1,2,0:T(8,128)(2,1)S(1)}, bf16[2,64,2,128]{3,1,2,0:T(8,128)(2,1)S(1)}, u32[]{:S(2)}, u32[]{:S(2)}) collective-permute-start(bf16[2,64,2,128]{3,1,2,0:T(8,128)(2,1)S(1)} %get-tuple-element.8), channel_id=1, source_target_pairs={{0,10},{2,12},{4,14},{6,0},{8,2},{10,4},{12,6},{14,8},{1,11},{3,13... | collective-permute-start | bytes 196616 | tf_op jit(solution)/shard_map/ppermute | solution.py:23
  12.1 5.7 %collective-permute-start.5 = (bf16[2,64,2,128]{3,1,2,0:T(8,128)(2,1)S(1)}, bf16[2,64,2,128]{3,1,2,0:T(8,128)(2,1)S(1)}, u32[]{:S(2)}, u32[]{:S(2)}) collective-permute-start(bf16[2,64,2,128]{3,1,2,0:T(8,128)(2,1)S(1)} %get-tuple-element.8), channel_id=1, source_target_pairs={{0,12},{2,14},{4,0},{6,2},{8,4},{10,6},{12,8},{14,10},{1,13},{3,15... | collective-permute-start | bytes 196616 | tf_op jit(solution)/shard_map/ppermute | solution.py:23
  13.5 4.3 %collective-permute-start.6 = (bf16[2,64,2,128]{3,1,2,0:T(8,128)(2,1)S(1)}, bf16[2,64,2,128]{3,1,2,0:T(8,128)(2,1)S(1)}, u32[]{:S(2)}, u32[]{:S(2)}) collective-permute-start(bf16[2,64,2,128]{3,1,2,0:T(8,128)(2,1)S(1)} %get-tuple-element.8), channel_id=1, source_target_pairs={{0,14},{2,0},{4,2},{6,4},{8,6},{10,8},{12,10},{14,12},{1,15},{3,1}... | collective-permute-start | bytes 196616 | tf_op jit(solution)/shard_map/ppermute | solution.py:23

commit v4 on v3

--- a/solution.py
+++ b/solution.py
@@ -1,6 +1,7 @@
 import jax
 import jax.numpy as jnp
 from jax import lax
+from jax.experimental.layout import Layout, with_layout_constraint
 from jax.sharding import PartitionSpec as P
 
 
@@ -37,6 +38,7 @@
     total = jnp.sum(weights, axis=-1)
     summed = jnp.einsum("hgqk,khd->hgqd", weights.astype(jnp.bfloat16), value_all,
                         preferred_element_type=jnp.float32)
+    summed = with_layout_constraint(summed, Layout((2, 0, 1, 3)))
     result = summed / total[..., None]
     result = jnp.transpose(result, (2, 0, 1, 3)).reshape(local_rows, query_heads, head_size)
     return result.astype(jnp.bfloat16)

time: 20.7 us -> 20.4 us (0.986)
  matrix products: 1.11 us -> 2.29 us
  local copies, waits for them, and re-layouts: 1.89 us -> 1.12 us
  other arithmetic: 0.78 us -> 0.13 us
    convert_element_type x1 -> x0, local copies, waits for them, and re-layouts: 0.88 us -> none  [per_device(): return result.astype(jnp.bfloat16)]
    dot_general x1, matrix products: 0.58 us -> 1.45 us  [per_device(): jnp.einsum('hgqk,khd->hgqd', weights.astype(jnp.bfloat16), value_all, pre...]
    sub x0 -> x1, matrix products: none -> 0.84 us  [per_device(): weights = jnp.exp(scores - row_max[..., None])]
    reduce_sum x1 -> x0, other arithmetic: 0.65 us -> none  [per_device(): total = jnp.sum(weights, axis=-1)]
    dot_general x1 -> x0, matrix products: 0.54 us -> none  [per_device(): jnp.einsum('qhgd,khd->hgqk', rows, key_all, preferred_element_type=jnp.fl...]
where the time goes in v4:
time: 20.4 us; the launch traced here: 20.3 us
  starting transfers between devices  13.8 us (68%)
  waiting for transfers between devices  2.79 us (14%)
  matrix products  2.29 us (11%)
  local copies, waits for them, and re-layouts  1.12 us (5%)
    ppermute x7, starting transfers between devices, per_device(): lax.ppermute(operand, 'ctx', [(i, (i + shift) % context_size) for i in ra...  13.8 us
    ppermute x7, waiting for transfers between devices, per_device(): lax.ppermute(operand, 'ctx', [(i, (i + shift) % context_size) for i in ra...  2.79 us
    dot_general x1, matrix products, per_device(): jnp.einsum('hgqk,khd->hgqd', weights.astype(jnp.bfloat16), value_all, pre...  1.45 us
    sub x1, matrix products, per_device(): weights = jnp.exp(scores - row_max[..., None])  0.84 us
    another operation x1, local copies, waits for them, and re-layouts, per_device(): pair = jnp.stack([keys, values], axis=0)  0.83 us
  transfers between devices with their start and end apart: 7, of which 2 were waited for; matrix products, arithmetic and copies ran while one was open for 1% of the time, Pallas kernels for 0%

profile of v4, /device:TPU:0, one launch (start us, length us, event | category | flops | bytes accessed | tf_op | source)
XLA Modules:
  0.0 20.3 jit_solution(9684921572171088879)
XLA Ops:
  0.0 0.0 copy-start
  0.0 0.8 %copy_bitcast_fusion = (bf16[1,64,2,128]{3,1,2,0:T(8,128)(2,1)S(1)}, bf16[1,64,2,128]{3,1,2,0:T(8,128)(2,1)S(1)}) fusion(bf16[64,2,128]{2,1,0:T(2,128)(2,1)} %param.5, bf16[64,2,128]{2,1,0:T(2,128)(2,1)} %param.4), kind=kLoop, calls=%fused_computation.17 | loop fusion | bytes 131072 | tf_op jit(solution)/shard_map/stack | solution.py:17
  0.9 3.0 %collective-permute-start.4 = (bf16[2,64,2,128]{3,1,2,0:T(8,128)(2,1)S(1)}, bf16[2,64,2,128]{3,1,2,0:T(8,128)(2,1)S(1)}, u32[]{:S(2)}, u32[]{:S(2)}) collective-permute-start(bf16[2,64,2,128]{3,1,2,0:T(8,128)(2,1)S(1)} %get-tuple-element.8), channel_id=1, source_target_pairs={{0,2},{2,4},{4,6},{6,8},{8,10},{10,12},{12,14},{14,0},{1,3},{3,5},... | collective-permute-start | bytes 196616 | tf_op jit(solution)/shard_map/ppermute | solution.py:24
  3.9 1.6 %collective-permute-start.3 = (bf16[2,64,2,128]{3,1,2,0:T(8,128)(2,1)S(1)}, bf16[2,64,2,128]{3,1,2,0:T(8,128)(2,1)S(1)}, u32[]{:S(2)}, u32[]{:S(2)}) collective-permute-start(bf16[2,64,2,128]{3,1,2,0:T(8,128)(2,1)S(1)} %get-tuple-element.8), channel_id=1, source_target_pairs={{0,4},{2,6},{4,8},{6,10},{8,12},{10,14},{12,0},{14,2},{1,5},{3,7},... | collective-permute-start | bytes 196616 | tf_op jit(solution)/shard_map/ppermute | solution.py:24
  5.5 2.6 %collective-permute-start.2 = (bf16[2,64,2,128]{3,1,2,0:T(8,128)(2,1)S(1)}, bf16[2,64,2,128]{3,1,2,0:T(8,128)(2,1)S(1)}, u32[]{:S(2)}, u32[]{:S(2)}) collective-permute-start(bf16[2,64,2,128]{3,1,2,0:T(8,128)(2,1)S(1)} %get-tuple-element.8), channel_id=1, source_target_pairs={{0,6},{2,8},{4,10},{6,12},{8,14},{10,0},{12,2},{14,4},{1,7},{3,9},... | collective-permute-start | bytes 196616 | tf_op jit(solution)/shard_map/ppermute | solution.py:24
  8.0 1.2 %collective-permute-start.1 = (bf16[2,64,2,128]{3,1,2,0:T(8,128)(2,1)S(1)}, bf16[2,64,2,128]{3,1,2,0:T(8,128)(2,1)S(1)}, u32[]{:S(2)}, u32[]{:S(2)}) collective-permute-start(bf16[2,64,2,128]{3,1,2,0:T(8,128)(2,1)S(1)} %get-tuple-element.8), channel_id=1, source_target_pairs={{0,8},{2,10},{4,12},{6,14},{8,0},{10,2},{12,4},{14,6},{1,9},{3,11}... | collective-permute-start | bytes 196616 | tf_op jit(solution)/shard_map/ppermute | solution.py:24
  9.3 2.6 %collective-permute-start = (bf16[2,64,2,128]{3,1,2,0:T(8,128)(2,1)S(1)}, bf16[2,64,2,128]{3,1,2,0:T(8,128)(2,1)S(1)}, u32[]{:S(2)}, u32[]{:S(2)}) collective-permute-start(bf16[2,64,2,128]{3,1,2,0:T(8,128)(2,1)S(1)} %get-tuple-element.8), channel_id=1, source_target_pairs={{0,10},{2,12},{4,14},{6,0},{8,2},{10,4},{12,6},{14,8},{1,11},{3,13... | collective-permute-start | bytes 196616 | tf_op jit(solution)/shard_map/ppermute | solution.py:24
  11.9 0.1 concatenate.6
  12.0 0.1 broadcast_compare_fusion
  12.1 0.0 collective-permute-done.4
  12.1 1.4 %collective-permute-start.5 = (bf16[2,64,2,128]{3,1,2,0:T(8,128)(2,1)S(1)}, bf16[2,64,2,128]{3,1,2,0:T(8,128)(2,1)S(1)}, u32[]{:S(2)}, u32[]{:S(2)}) collective-permute-start(bf16[2,64,2,128]{3,1,2,0:T(8,128)(2,1)S(1)} %get-tuple-element.8), channel_id=1, source_target_pairs={{0,12},{2,14},{4,0},{6,2},{8,4},{10,6},{12,8},{14,10},{1,13},{3,15... | collective-permute-start | bytes 196616 | tf_op jit(solution)/shard_map/ppermute | solution.py:24
  13.5 0.0 collective-permute-done.3
  13.5 1.4 %collective-permute-start.6 = (bf16[2,64,2,128]{3,1,2,0:T(8,128)(2,1)S(1)}, bf16[2,64,2,128]{3,1,2,0:T(8,128)(2,1)S(1)}, u32[]{:S(2)}, u32[]{:S(2)}) collective-permute-start(bf16[2,64,2,128]{3,1,2,0:T(8,128)(2,1)S(1)} %get-tuple-element.8), channel_id=1, source_target_pairs={{0,14},{2,0},{4,2},{6,4},{8,6},{10,8},{12,10},{14,12},{1,15},{3,1}... | collective-permute-start | bytes 196616 | tf_op jit(solution)/shard_map/ppermute | solution.py:24
  14.9 1.8 %collective-permute-done = bf16[2,64,2,128]{3,1,2,0:T(8,128)(2,1)S(1)} collective-permute-done((bf16[2,64,2,128]{3,1,2,0:T(8,128)(2,1)S(1)}, bf16[2,64,2,128]{3,1,2,0:T(8,128)(2,1)S(1)}, u32[]{:S(2)}, u32[]{:S(2)}) %collective-permute-start) | collective-permute-done | bytes 65568 | tf_op jit(solution)/shard_map/ppermute | solution.py:24
  16.8 0.0 collective-permute-done.1
  16.8 0.0 collective-permute-done.2
  16.9 1.0 %collective-permute-done.5 = bf16[2,64,2,128]{3,1,2,0:T(8,128)(2,1)S(1)} collective-permute-done((bf16[2,64,2,128]{3,1,2,0:T(8,128)(2,1)S(1)}, bf16[2,64,2,128]{3,1,2,0:T(8,128)(2,1)S(1)}, u32[]{:S(2)}, u32[]{:S(2)}) %collective-permute-start.5) | collective-permute-done | bytes 65568 | tf_op jit(solution)/shard_map/ppermute | solution.py:24
  17.8 0.0 collective-permute-done.6
  17.9 0.0 copy-done
  17.9 0.8 %fusion.18 = (f32[2,8,64]{2,1,0:T(8,128)S(1)}, bf16[2,8,64,512]{3,2,1,0:T(8,128)(2,1)S(1)}) fusion(pred[64,512]{1,0:T(8,128)(4,1)S(1)} %broadcast_compare_fusion, bf16[64,2,8,128]{3,2,1,0:T(8,128)(2,1)S(1)} %bitcast.34, bf16[2,512,2,128]{3,1,2,0:T(8,128)(2,1)S(1)} %constant_dynamic-update-slice_fusion), kind=kOutput, calls=%fused_computation.37 | convolution fusion | flops 136839680 | bytes 1609728 | tf_op jit(solution)/shard_map/sub | solution.py:37
  18.7 0.1 copy.12
  18.8 1.4 %fusion.3 = bf16[64,16,128]{2,1,0:T(8,128)(2,1)} fusion(bf16[2,8,64,512]{3,2,1,0:T(8,128)(2,1)S(1)} %get-tuple-element.10, bf16[2,512,2,128]{3,1,2,0:T(8,128)(2,1)S(1)} %constant_dynamic-update-slice_fusion, f32[2,8,64]{1,0,2:T(2,128)S(1)} %copy.12), kind=kOutput, calls=%fused_computation.6 | convolution fusion | flops 134479872 | bytes 1638400 | tf_op jit(solution)/shard_map/hgqk,khd->hgqd/dot_general | solution.py:39
  (13 shorter events, 0.1 us)
Async XLA Ops:
  0.0 17.9 %copy-start = (bf16[64,16,128]{2,1,0:T(8,128)(2,1)S(1)}, bf16[64,16,128]{2,1,0:T(8,128)(2,1)}, u32[]{:S(2)}) copy-start(bf16[64,16,128]{2,1,0:T(8,128)(2,1)} %param.3) | copy-start | bytes 786436
  0.9 11.2 %collective-permute-start.4 = (bf16[2,64,2,128]{3,1,2,0:T(8,128)(2,1)S(1)}, bf16[2,64,2,128]{3,1,2,0:T(8,128)(2,1)S(1)}, u32[]{:S(2)}, u32[]{:S(2)}) collective-permute-start(bf16[2,64,2,128]{3,1,2,0:T(8,128)(2,1)S(1)} %get-tuple-element.8), channel_id=1, source_target_pairs={{0,2},{2,4},{4,6},{6,8},{8,10},{10,12},{12,14},{14,0},{1,3},{3,5},... | collective-permute-start | bytes 196616 | tf_op jit(solution)/shard_map/ppermute | solution.py:24
  3.9 9.6 %collective-permute-start.3 = (bf16[2,64,2,128]{3,1,2,0:T(8,128)(2,1)S(1)}, bf16[2,64,2,128]{3,1,2,0:T(8,128)(2,1)S(1)}, u32[]{:S(2)}, u32[]{:S(2)}) collective-permute-start(bf16[2,64,2,128]{3,1,2,0:T(8,128)(2,1)S(1)} %get-tuple-element.8), channel_id=1, source_target_pairs={{0,4},{2,6},{4,8},{6,10},{8,12},{10,14},{12,0},{14,2},{1,5},{3,7},... | collective-permute-start | bytes 196616 | tf_op jit(solution)/shard_map/ppermute | solution.py:24
  5.5 11.3 %collective-permute-start.2 = (bf16[2,64,2,128]{3,1,2,0:T(8,128)(2,1)S(1)}, bf16[2,64,2,128]{3,1,2,0:T(8,128)(2,1)S(1)}, u32[]{:S(2)}, u32[]{:S(2)}) collective-permute-start(bf16[2,64,2,128]{3,1,2,0:T(8,128)(2,1)S(1)} %get-tuple-element.8), channel_id=1, source_target_pairs={{0,6},{2,8},{4,10},{6,12},{8,14},{10,0},{12,2},{14,4},{1,7},{3,9},... | collective-permute-start | bytes 196616 | tf_op jit(solution)/shard_map/ppermute | solution.py:24
  8.0 8.7 %collective-permute-start.1 = (bf16[2,64,2,128]{3,1,2,0:T(8,128)(2,1)S(1)}, bf16[2,64,2,128]{3,1,2,0:T(8,128)(2,1)S(1)}, u32[]{:S(2)}, u32[]{:S(2)}) collective-permute-start(bf16[2,64,2,128]{3,1,2,0:T(8,128)(2,1)S(1)} %get-tuple-element.8), channel_id=1, source_target_pairs={{0,8},{2,10},{4,12},{6,14},{8,0},{10,2},{12,4},{14,6},{1,9},{3,11}... | collective-permute-start | bytes 196616 | tf_op jit(solution)/shard_map/ppermute | solution.py:24
  9.3 7.5 %collective-permute-start = (bf16[2,64,2,128]{3,1,2,0:T(8,128)(2,1)S(1)}, bf16[2,64,2,128]{3,1,2,0:T(8,128)(2,1)S(1)}, u32[]{:S(2)}, u32[]{:S(2)}) collective-permute-start(bf16[2,64,2,128]{3,1,2,0:T(8,128)(2,1)S(1)} %get-tuple-element.8), channel_id=1, source_target_pairs={{0,10},{2,12},{4,14},{6,0},{8,2},{10,4},{12,6},{14,8},{1,11},{3,13... | collective-permute-start | bytes 196616 | tf_op jit(solution)/shard_map/ppermute | solution.py:24
  12.1 5.7 %collective-permute-start.5 = (bf16[2,64,2,128]{3,1,2,0:T(8,128)(2,1)S(1)}, bf16[2,64,2,128]{3,1,2,0:T(8,128)(2,1)S(1)}, u32[]{:S(2)}, u32[]{:S(2)}) collective-permute-start(bf16[2,64,2,128]{3,1,2,0:T(8,128)(2,1)S(1)} %get-tuple-element.8), channel_id=1, source_target_pairs={{0,12},{2,14},{4,0},{6,2},{8,4},{10,6},{12,8},{14,10},{1,13},{3,15... | collective-permute-start | bytes 196616 | tf_op jit(solution)/shard_map/ppermute | solution.py:24
  13.5 4.3 %collective-permute-start.6 = (bf16[2,64,2,128]{3,1,2,0:T(8,128)(2,1)S(1)}, bf16[2,64,2,128]{3,1,2,0:T(8,128)(2,1)S(1)}, u32[]{:S(2)}, u32[]{:S(2)}) collective-permute-start(bf16[2,64,2,128]{3,1,2,0:T(8,128)(2,1)S(1)} %get-tuple-element.8), channel_id=1, source_target_pairs={{0,14},{2,0},{4,2},{6,4},{8,6},{10,8},{12,10},{14,12},{1,15},{3,1}... | collective-permute-start | bytes 196616 | tf_op jit(solution)/shard_map/ppermute | solution.py:24

commit v5 on v4

--- a/solution.py
+++ b/solution.py
@@ -33,7 +33,17 @@
     scores = jnp.einsum("qhgd,khd->hgqk", rows, key_all, preferred_element_type=jnp.float32) * scale
     valid = key_position[None, :] <= position[:, None]
     scores = jnp.where(valid, scores, -1e30)
-    row_max = jnp.max(scores, axis=-1)
+    early = [1, 2] if context_size == 8 else []
+    late = [3, 4, 5, 6, 7] if context_size == 8 else [shift for shift in order if shift not in early]
+    part_max = []
+    for part in ([0] + early, late):
+        part_keys = jnp.concatenate([pieces[0] if shift == 0 else moved[shift] for shift in part], axis=1)[0]
+        part_position = jnp.concatenate(
+            [((me - shift) % context_size) * local_rows + offset for shift in part], axis=0)
+        part_scores = jnp.einsum("qhgd,khd->hgqk", rows, part_keys, preferred_element_type=jnp.float32) * scale
+        part_valid = part_position[None, :] <= position[:, None]
+        part_max.append(jnp.max(jnp.where(part_valid, part_scores, -1e30), axis=-1))
+    row_max = jnp.maximum(part_max[0], part_max[1])
     weights = jnp.exp(scores - row_max[..., None])
     total = jnp.sum(weights, axis=-1)
     summed = jnp.einsum("hgqk,khd->hgqd", weights.astype(jnp.bfloat16), value_all,

time: 20.4 us -> 21.2 us (1.039)
  matrix products: 2.29 us -> 3.09 us
  waiting for transfers between devices: 2.79 us -> 2.3 us
  other arithmetic: 0.13 us -> 0.37 us
    dot_general x0 -> x3, matrix products: none -> 1.64 us  [the longest x2 0.86 us: per_device(): jnp.einsum('qhgd,khd->hgqk', rows, part_keys, preferred_element_type=jnp....]
    sub x1 -> x0, matrix products: 0.84 us -> none  [per_device(): weights = jnp.exp(scores - row_max[..., None])]
    ppermute x7, waiting for transfers between devices: 2.79 us -> 2.3 us  [per_device(): lax.ppermute(operand, 'ctx', [(i, (i + shift) % context_size) for i in ra...]
  transfers between devices with their start and end apart: 7 -> 7, of which waited for: 2 -> 2; matrix products, arithmetic and copies ran while one was open for 1% -> 5% of each run, Pallas kernels for 0% -> 0%
where the time goes in v5:
time: 21.2 us; the launch traced here: 21 us
  starting transfers between devices  13.8 us (65%)
  matrix products  3.09 us (15%)
  waiting for transfers between devices  2.3 us (11%)
  local copies, waits for them, and re-layouts  1.27 us (6%)
  other arithmetic  0.37 us (2%)
    ppermute x7, starting transfers between devices, per_device(): lax.ppermute(operand, 'ctx', [(i, (i + shift) % context_size) for i in ra...  13.8 us
    ppermute x7, waiting for transfers between devices, per_device(): lax.ppermute(operand, 'ctx', [(i, (i + shift) % context_size) for i in ra...  2.3 us
    dot_general x1, matrix products, per_device(): jnp.einsum('hgqk,khd->hgqd', weights.astype(jnp.bfloat16), value_all, pre...  1.45 us
    dot_general x2, matrix products, per_device(): jnp.einsum('qhgd,khd->hgqk', rows, part_keys, preferred_element_type=jnp....  0.86 us
    another operation x1, local copies, waits for them, and re-layouts, per_device(): pair = jnp.stack([keys, values], axis=0)  0.83 us
    dot_general x1, matrix products, per_device(): jnp.einsum('qhgd,khd->hgqk', rows, key_all, preferred_element_type=jnp.fl...  0.79 us
  transfers between devices with their start and end apart: 7, of which 2 were waited for; matrix products, arithmetic and copies ran while one was open for 5% of the time, Pallas kernels for 0%

profile of v5, /device:TPU:0, one launch (start us, length us, event | category | flops | bytes accessed | tf_op | source)
XLA Modules:
  0.0 21.0 jit_solution(3481501856187587100)
XLA Ops:
  0.0 0.8 %copy_bitcast_fusion = (bf16[1,64,2,128]{3,1,2,0:T(8,128)(2,1)S(1)}, bf16[1,64,2,128]{3,1,2,0:T(8,128)(2,1)S(1)}) fusion(bf16[64,2,128]{2,1,0:T(2,128)(2,1)} %param.5, bf16[64,2,128]{2,1,0:T(2,128)(2,1)} %param.4), kind=kLoop, calls=%fused_computation.27 | loop fusion | bytes 131072 | tf_op jit(solution)/shard_map/stack | solution.py:17
  0.9 3.0 %collective-permute-start.4 = (bf16[2,64,2,128]{3,1,2,0:T(8,128)(2,1)S(1)}, bf16[2,64,2,128]{3,1,2,0:T(8,128)(2,1)S(1)}, u32[]{:S(2)}, u32[]{:S(2)}) collective-permute-start(bf16[2,64,2,128]{3,1,2,0:T(8,128)(2,1)S(1)} %get-tuple-element.8), channel_id=1, source_target_pairs={{0,2},{2,4},{4,6},{6,8},{8,10},{10,12},{12,14},{14,0},{1,3},{3,5},... | collective-permute-start | bytes 196616 | tf_op jit(solution)/shard_map/ppermute | solution.py:24
  3.9 1.6 %collective-permute-start.3 = (bf16[2,64,2,128]{3,1,2,0:T(8,128)(2,1)S(1)}, bf16[2,64,2,128]{3,1,2,0:T(8,128)(2,1)S(1)}, u32[]{:S(2)}, u32[]{:S(2)}) collective-permute-start(bf16[2,64,2,128]{3,1,2,0:T(8,128)(2,1)S(1)} %get-tuple-element.8), channel_id=1, source_target_pairs={{0,4},{2,6},{4,8},{6,10},{8,12},{10,14},{12,0},{14,2},{1,5},{3,7},... | collective-permute-start | bytes 196616 | tf_op jit(solution)/shard_map/ppermute | solution.py:24
  5.5 2.6 %collective-permute-start.2 = (bf16[2,64,2,128]{3,1,2,0:T(8,128)(2,1)S(1)}, bf16[2,64,2,128]{3,1,2,0:T(8,128)(2,1)S(1)}, u32[]{:S(2)}, u32[]{:S(2)}) collective-permute-start(bf16[2,64,2,128]{3,1,2,0:T(8,128)(2,1)S(1)} %get-tuple-element.8), channel_id=1, source_target_pairs={{0,6},{2,8},{4,10},{6,12},{8,14},{10,0},{12,2},{14,4},{1,7},{3,9},... | collective-permute-start | bytes 196616 | tf_op jit(solution)/shard_map/ppermute | solution.py:24
  8.0 1.2 %collective-permute-start.1 = (bf16[2,64,2,128]{3,1,2,0:T(8,128)(2,1)S(1)}, bf16[2,64,2,128]{3,1,2,0:T(8,128)(2,1)S(1)}, u32[]{:S(2)}, u32[]{:S(2)}) collective-permute-start(bf16[2,64,2,128]{3,1,2,0:T(8,128)(2,1)S(1)} %get-tuple-element.8), channel_id=1, source_target_pairs={{0,8},{2,10},{4,12},{6,14},{8,0},{10,2},{12,4},{14,6},{1,9},{3,11}... | collective-permute-start | bytes 196616 | tf_op jit(solution)/shard_map/ppermute | solution.py:24
  9.3 2.6 %collective-permute-start = (bf16[2,64,2,128]{3,1,2,0:T(8,128)(2,1)S(1)}, bf16[2,64,2,128]{3,1,2,0:T(8,128)(2,1)S(1)}, u32[]{:S(2)}, u32[]{:S(2)}) collective-permute-start(bf16[2,64,2,128]{3,1,2,0:T(8,128)(2,1)S(1)} %get-tuple-element.8), channel_id=1, source_target_pairs={{0,10},{2,12},{4,14},{6,0},{8,2},{10,4},{12,6},{14,8},{1,11},{3,13... | collective-permute-start | bytes 196616 | tf_op jit(solution)/shard_map/ppermute | solution.py:24
  11.9 0.1 pad_add_fusion
  12.0 0.1 concatenate.22
  12.1 0.1 concatenate.18
  12.1 0.1 broadcast_compare_fusion.1
  12.2 0.1 broadcast_compare_fusion
  12.3 0.1 broadcast_compare_fusion.2
  12.4 0.0 collective-permute-done.4
  12.4 1.4 %collective-permute-start.5 = (bf16[2,64,2,128]{3,1,2,0:T(8,128)(2,1)S(1)}, bf16[2,64,2,128]{3,1,2,0:T(8,128)(2,1)S(1)}, u32[]{:S(2)}, u32[]{:S(2)}) collective-permute-start(bf16[2,64,2,128]{3,1,2,0:T(8,128)(2,1)S(1)} %get-tuple-element.8), channel_id=1, source_target_pairs={{0,12},{2,14},{4,0},{6,2},{8,4},{10,6},{12,8},{14,10},{1,13},{3,15... | collective-permute-start | bytes 196616 | tf_op jit(solution)/shard_map/ppermute | solution.py:24
  13.8 0.0 collective-permute-done.3
  13.8 1.4 %collective-permute-start.6 = (bf16[2,64,2,128]{3,1,2,0:T(8,128)(2,1)S(1)}, bf16[2,64,2,128]{3,1,2,0:T(8,128)(2,1)S(1)}, u32[]{:S(2)}, u32[]{:S(2)}) collective-permute-start(bf16[2,64,2,128]{3,1,2,0:T(8,128)(2,1)S(1)} %get-tuple-element.8), channel_id=1, source_target_pairs={{0,14},{2,0},{4,2},{6,4},{8,6},{10,8},{12,10},{14,12},{1,15},{3,1}... | collective-permute-start | bytes 196616 | tf_op jit(solution)/shard_map/ppermute | solution.py:24
  15.3 1.6 %collective-permute-done = bf16[2,64,2,128]{3,1,2,0:T(8,128)(2,1)S(1)} collective-permute-done((bf16[2,64,2,128]{3,1,2,0:T(8,128)(2,1)S(1)}, bf16[2,64,2,128]{3,1,2,0:T(8,128)(2,1)S(1)}, u32[]{:S(2)}, u32[]{:S(2)}) %collective-permute-start) | collective-permute-done | bytes 65568 | tf_op jit(solution)/shard_map/ppermute | solution.py:24
  17.1 0.4 %fusion.5 = f32[2,8,64]{2,1,0:T(8,128)S(1)} fusion(pred[64,192]{1,0:T(8,128)(4,1)S(1)} %broadcast_compare_fusion.2, bf16[64,2,8,128]{3,2,1,0:T(8,128)(2,1)S(1)} %bitcast.51, bf16[2,64,2,128]{3,1,2,0:T(8,128)(2,1)S(1)} %collective-permute-done.3, bf16[2,64,2,128]{3,1,2,0:T(8,128)(2,1)S(1)} %collective-permute-done.4, ...), kind=kOutput, calls=%fused_computation.8 | convolution fusion | flops 51313664 | bytes 475136 | tf_op jit(solution)/shard_map/qhgd,khd->hgqk/dot_general | solution.py:43
  17.5 0.6 %collective-permute-done.5 = bf16[2,64,2,128]{3,1,2,0:T(8,128)(2,1)S(1)} collective-permute-done((bf16[2,64,2,128]{3,1,2,0:T(8,128)(2,1)S(1)}, bf16[2,64,2,128]{3,1,2,0:T(8,128)(2,1)S(1)}, u32[]{:S(2)}, u32[]{:S(2)}) %collective-permute-start.5) | collective-permute-done | bytes 65568 | tf_op jit(solution)/shard_map/ppermute | solution.py:24
  18.2 0.0 collective-permute-done.6
  18.2 0.5 %fusion.2 = f32[2,8,64]{2,1,0:T(8,128)S(1)} fusion(pred[64,320]{1,0:T(8,128)(4,1)S(1)} %broadcast_compare_fusion.1, bf16[64,2,8,128]{3,2,1,0:T(8,128)(2,1)S(1)} %bitcast.50, bf16[2,320,2,128]{3,1,2,0:T(8,128)(2,1)S(1)} %get-tuple-element.12), kind=kOutput, calls=%fused_computation.4 | convolution fusion | flops 84868096 | bytes 454656 | tf_op jit(solution)/shard_map/qhgd,khd->hgqk/dot_general | solution.py:43
  18.7 0.8 %fusion.16 = (f32[2,8,64]{2,1,0:T(8,128)S(1)}, bf16[2,8,64,512]{3,2,1,0:T(8,128)(2,1)S(1)}) fusion(f32[2,8,64]{2,1,0:T(8,128)S(1)} %max.7, bf16[64,2,8,128]{3,2,1,0:T(8,128)(2,1)S(1)} %bitcast.49, bf16[2,512,2,128]{3,1,2,0:T(8,128)(2,1)S(1)} %get-tuple-element.11, pred[64,512]{1,0:T(8,128)(4,1)S(1)} %broadcast_compare_fusion), kind=kOutput, calls=%fused_computation.54 | convolution fusion | flops 136838144 | bytes 1617920 | tf_op jit(solution)/shard_map/qhgd,khd->hgqk/dot_general | solution.py:33
  19.5 0.1 copy.16
  19.6 1.4 %fusion.7 = bf16[64,16,128]{2,1,0:T(8,128)(2,1)} fusion(bf16[2,8,64,512]{3,2,1,0:T(8,128)(2,1)S(1)} %get-tuple-element.10, bf16[2,512,2,128]{3,1,2,0:T(8,128)(2,1)S(1)} %get-tuple-element.11, f32[2,8,64]{1,0,2:T(2,128)S(1)} %copy.16), kind=kOutput, calls=%fused_computation.11 | convolution fusion | flops 134479872 | bytes 1638400 | tf_op jit(solution)/shard_map/hgqk,khd->hgqd/dot_general | solution.py:49
  (20 shorter events, 0.2 us)
Async XLA Ops:
  0.0 17.1 %copy-start = (bf16[64,16,128]{2,1,0:T(8,128)(2,1)S(1)}, bf16[64,16,128]{2,1,0:T(8,128)(2,1)}, u32[]{:S(2)}) copy-start(bf16[64,16,128]{2,1,0:T(8,128)(2,1)} %param.3) | copy-start | bytes 786436
  0.9 11.6 %collective-permute-start.4 = (bf16[2,64,2,128]{3,1,2,0:T(8,128)(2,1)S(1)}, bf16[2,64,2,128]{3,1,2,0:T(8,128)(2,1)S(1)}, u32[]{:S(2)}, u32[]{:S(2)}) collective-permute-start(bf16[2,64,2,128]{3,1,2,0:T(8,128)(2,1)S(1)} %get-tuple-element.8), channel_id=1, source_target_pairs={{0,2},{2,4},{4,6},{6,8},{8,10},{10,12},{12,14},{14,0},{1,3},{3,5},... | collective-permute-start | bytes 196616 | tf_op jit(solution)/shard_map/ppermute | solution.py:24
  3.9 9.9 %collective-permute-start.3 = (bf16[2,64,2,128]{3,1,2,0:T(8,128)(2,1)S(1)}, bf16[2,64,2,128]{3,1,2,0:T(8,128)(2,1)S(1)}, u32[]{:S(2)}, u32[]{:S(2)}) collective-permute-start(bf16[2,64,2,128]{3,1,2,0:T(8,128)(2,1)S(1)} %get-tuple-element.8), channel_id=1, source_target_pairs={{0,4},{2,6},{4,8},{6,10},{8,12},{10,14},{12,0},{14,2},{1,5},{3,7},... | collective-permute-start | bytes 196616 | tf_op jit(solution)/shard_map/ppermute | solution.py:24
  5.5 11.5 %collective-permute-start.2 = (bf16[2,64,2,128]{3,1,2,0:T(8,128)(2,1)S(1)}, bf16[2,64,2,128]{3,1,2,0:T(8,128)(2,1)S(1)}, u32[]{:S(2)}, u32[]{:S(2)}) collective-permute-start(bf16[2,64,2,128]{3,1,2,0:T(8,128)(2,1)S(1)} %get-tuple-element.8), channel_id=1, source_target_pairs={{0,6},{2,8},{4,10},{6,12},{8,14},{10,0},{12,2},{14,4},{1,7},{3,9},... | collective-permute-start | bytes 196616 | tf_op jit(solution)/shard_map/ppermute | solution.py:24
  8.0 8.9 %collective-permute-start.1 = (bf16[2,64,2,128]{3,1,2,0:T(8,128)(2,1)S(1)}, bf16[2,64,2,128]{3,1,2,0:T(8,128)(2,1)S(1)}, u32[]{:S(2)}, u32[]{:S(2)}) collective-permute-start(bf16[2,64,2,128]{3,1,2,0:T(8,128)(2,1)S(1)} %get-tuple-element.8), channel_id=1, source_target_pairs={{0,8},{2,10},{4,12},{6,14},{8,0},{10,2},{12,4},{14,6},{1,9},{3,11}... | collective-permute-start | bytes 196616 | tf_op jit(solution)/shard_map/ppermute | solution.py:24
  9.3 7.7 %collective-permute-start = (bf16[2,64,2,128]{3,1,2,0:T(8,128)(2,1)S(1)}, bf16[2,64,2,128]{3,1,2,0:T(8,128)(2,1)S(1)}, u32[]{:S(2)}, u32[]{:S(2)}) collective-permute-start(bf16[2,64,2,128]{3,1,2,0:T(8,128)(2,1)S(1)} %get-tuple-element.8), channel_id=1, source_target_pairs={{0,10},{2,12},{4,14},{6,0},{8,2},{10,4},{12,6},{14,8},{1,11},{3,13... | collective-permute-start | bytes 196616 | tf_op jit(solution)/shard_map/ppermute | solution.py:24
  12.4 5.7 %collective-permute-start.5 = (bf16[2,64,2,128]{3,1,2,0:T(8,128)(2,1)S(1)}, bf16[2,64,2,128]{3,1,2,0:T(8,128)(2,1)S(1)}, u32[]{:S(2)}, u32[]{:S(2)}) collective-permute-start(bf16[2,64,2,128]{3,1,2,0:T(8,128)(2,1)S(1)} %get-tuple-element.8), channel_id=1, source_target_pairs={{0,12},{2,14},{4,0},{6,2},{8,4},{10,6},{12,8},{14,10},{1,13},{3,15... | collective-permute-start | bytes 196616 | tf_op jit(solution)/shard_map/ppermute | solution.py:24
  13.8 4.3 %collective-permute-start.6 = (bf16[2,64,2,128]{3,1,2,0:T(8,128)(2,1)S(1)}, bf16[2,64,2,128]{3,1,2,0:T(8,128)(2,1)S(1)}, u32[]{:S(2)}, u32[]{:S(2)}) collective-permute-start(bf16[2,64,2,128]{3,1,2,0:T(8,128)(2,1)S(1)} %get-tuple-element.8), channel_id=1, source_target_pairs={{0,14},{2,0},{4,2},{6,4},{8,6},{10,8},{12,10},{14,12},{1,15},{3,1}... | collective-permute-start | bytes 196616 | tf_op jit(solution)/shard_map/ppermute | solution.py:24

commit v6 on v4

--- a/solution.py
+++ b/solution.py
@@ -30,11 +30,11 @@
     key_all = gathered[0]
     value_all = gathered[1]
     rows = queries.reshape(local_rows, key_heads, group_size, head_size)
-    scores = jnp.einsum("qhgd,khd->hgqk", rows, key_all, preferred_element_type=jnp.float32) * scale
+    scores = jnp.einsum("qhgd,khd->hgqk", rows, key_all, preferred_element_type=jnp.float32)
     valid = key_position[None, :] <= position[:, None]
     scores = jnp.where(valid, scores, -1e30)
     row_max = jnp.max(scores, axis=-1)
-    weights = jnp.exp(scores - row_max[..., None])
+    weights = jnp.exp((scores - row_max[..., None]) * scale)
     total = jnp.sum(weights, axis=-1)
     summed = jnp.einsum("hgqk,khd->hgqd", weights.astype(jnp.bfloat16), value_all,
                         preferred_element_type=jnp.float32)

time: 20.4 us -> 20.4 us (level)
  no operation moved by 1% of the time
where the time goes in v6:
time: 20.4 us; the launch traced here: 20.3 us
  starting transfers between devices  13.8 us (68%)
  waiting for transfers between devices  2.79 us (14%)
  matrix products  2.3 us (11%)
  local copies, waits for them, and re-layouts  1.12 us (5%)
    ppermute x7, starting transfers between devices, per_device(): lax.ppermute(operand, 'ctx', [(i, (i + shift) % context_size) for i in ra...  13.8 us
    ppermute x7, waiting for transfers between devices, per_device(): lax.ppermute(operand, 'ctx', [(i, (i + shift) % context_size) for i in ra...  2.79 us
    dot_general x1, matrix products, per_device(): jnp.einsum('hgqk,khd->hgqd', weights.astype(jnp.bfloat16), value_all, pre...  1.45 us
    sub x1, matrix products, per_device(): weights = jnp.exp((scores - row_max[..., None]) * scale)  0.85 us
    another operation x1, local copies, waits for them, and re-layouts, per_device(): pair = jnp.stack([keys, values], axis=0)  0.83 us
  transfers between devices with their start and end apart: 7, of which 2 were waited for; matrix products, arithmetic and copies ran while one was open for 1% of the time, Pallas kernels for 0%

profile of v6, /device:TPU:0, one launch (start us, length us, event | category | flops | bytes accessed | tf_op | source)
XLA Modules:
  0.0 20.3 jit_solution(17941990212316751209)
XLA Ops:
  0.0 0.0 copy-start
  0.0 0.8 %copy_bitcast_fusion = (bf16[1,64,2,128]{3,1,2,0:T(8,128)(2,1)S(1)}, bf16[1,64,2,128]{3,1,2,0:T(8,128)(2,1)S(1)}) fusion(bf16[64,2,128]{2,1,0:T(2,128)(2,1)} %param.5, bf16[64,2,128]{2,1,0:T(2,128)(2,1)} %param.4), kind=kLoop, calls=%fused_computation.16 | loop fusion | bytes 131072 | tf_op jit(solution)/shard_map/stack | solution.py:17
  0.9 3.0 %collective-permute-start.4 = (bf16[2,64,2,128]{3,1,2,0:T(8,128)(2,1)S(1)}, bf16[2,64,2,128]{3,1,2,0:T(8,128)(2,1)S(1)}, u32[]{:S(2)}, u32[]{:S(2)}) collective-permute-start(bf16[2,64,2,128]{3,1,2,0:T(8,128)(2,1)S(1)} %get-tuple-element.8), channel_id=1, source_target_pairs={{0,2},{2,4},{4,6},{6,8},{8,10},{10,12},{12,14},{14,0},{1,3},{3,5},... | collective-permute-start | bytes 196616 | tf_op jit(solution)/shard_map/ppermute | solution.py:24
  3.9 1.6 %collective-permute-start.3 = (bf16[2,64,2,128]{3,1,2,0:T(8,128)(2,1)S(1)}, bf16[2,64,2,128]{3,1,2,0:T(8,128)(2,1)S(1)}, u32[]{:S(2)}, u32[]{:S(2)}) collective-permute-start(bf16[2,64,2,128]{3,1,2,0:T(8,128)(2,1)S(1)} %get-tuple-element.8), channel_id=1, source_target_pairs={{0,4},{2,6},{4,8},{6,10},{8,12},{10,14},{12,0},{14,2},{1,5},{3,7},... | collective-permute-start | bytes 196616 | tf_op jit(solution)/shard_map/ppermute | solution.py:24
  5.5 2.6 %collective-permute-start.2 = (bf16[2,64,2,128]{3,1,2,0:T(8,128)(2,1)S(1)}, bf16[2,64,2,128]{3,1,2,0:T(8,128)(2,1)S(1)}, u32[]{:S(2)}, u32[]{:S(2)}) collective-permute-start(bf16[2,64,2,128]{3,1,2,0:T(8,128)(2,1)S(1)} %get-tuple-element.8), channel_id=1, source_target_pairs={{0,6},{2,8},{4,10},{6,12},{8,14},{10,0},{12,2},{14,4},{1,7},{3,9},... | collective-permute-start | bytes 196616 | tf_op jit(solution)/shard_map/ppermute | solution.py:24
  8.0 1.2 %collective-permute-start.1 = (bf16[2,64,2,128]{3,1,2,0:T(8,128)(2,1)S(1)}, bf16[2,64,2,128]{3,1,2,0:T(8,128)(2,1)S(1)}, u32[]{:S(2)}, u32[]{:S(2)}) collective-permute-start(bf16[2,64,2,128]{3,1,2,0:T(8,128)(2,1)S(1)} %get-tuple-element.8), channel_id=1, source_target_pairs={{0,8},{2,10},{4,12},{6,14},{8,0},{10,2},{12,4},{14,6},{1,9},{3,11}... | collective-permute-start | bytes 196616 | tf_op jit(solution)/shard_map/ppermute | solution.py:24
  9.3 2.6 %collective-permute-start = (bf16[2,64,2,128]{3,1,2,0:T(8,128)(2,1)S(1)}, bf16[2,64,2,128]{3,1,2,0:T(8,128)(2,1)S(1)}, u32[]{:S(2)}, u32[]{:S(2)}) collective-permute-start(bf16[2,64,2,128]{3,1,2,0:T(8,128)(2,1)S(1)} %get-tuple-element.8), channel_id=1, source_target_pairs={{0,10},{2,12},{4,14},{6,0},{8,2},{10,4},{12,6},{14,8},{1,11},{3,13... | collective-permute-start | bytes 196616 | tf_op jit(solution)/shard_map/ppermute | solution.py:24
  11.9 0.1 concatenate.6
  12.0 0.1 broadcast_compare_fusion
  12.1 0.0 collective-permute-done.4
  12.1 1.4 %collective-permute-start.5 = (bf16[2,64,2,128]{3,1,2,0:T(8,128)(2,1)S(1)}, bf16[2,64,2,128]{3,1,2,0:T(8,128)(2,1)S(1)}, u32[]{:S(2)}, u32[]{:S(2)}) collective-permute-start(bf16[2,64,2,128]{3,1,2,0:T(8,128)(2,1)S(1)} %get-tuple-element.8), channel_id=1, source_target_pairs={{0,12},{2,14},{4,0},{6,2},{8,4},{10,6},{12,8},{14,10},{1,13},{3,15... | collective-permute-start | bytes 196616 | tf_op jit(solution)/shard_map/ppermute | solution.py:24
  13.5 0.0 collective-permute-done.3
  13.5 1.4 %collective-permute-start.6 = (bf16[2,64,2,128]{3,1,2,0:T(8,128)(2,1)S(1)}, bf16[2,64,2,128]{3,1,2,0:T(8,128)(2,1)S(1)}, u32[]{:S(2)}, u32[]{:S(2)}) collective-permute-start(bf16[2,64,2,128]{3,1,2,0:T(8,128)(2,1)S(1)} %get-tuple-element.8), channel_id=1, source_target_pairs={{0,14},{2,0},{4,2},{6,4},{8,6},{10,8},{12,10},{14,12},{1,15},{3,1}... | collective-permute-start | bytes 196616 | tf_op jit(solution)/shard_map/ppermute | solution.py:24
  14.9 1.8 %collective-permute-done = bf16[2,64,2,128]{3,1,2,0:T(8,128)(2,1)S(1)} collective-permute-done((bf16[2,64,2,128]{3,1,2,0:T(8,128)(2,1)S(1)}, bf16[2,64,2,128]{3,1,2,0:T(8,128)(2,1)S(1)}, u32[]{:S(2)}, u32[]{:S(2)}) %collective-permute-start) | collective-permute-done | bytes 65568 | tf_op jit(solution)/shard_map/ppermute | solution.py:24
  16.8 0.0 collective-permute-done.1
  16.8 0.0 collective-permute-done.2
  16.9 1.0 %collective-permute-done.5 = bf16[2,64,2,128]{3,1,2,0:T(8,128)(2,1)S(1)} collective-permute-done((bf16[2,64,2,128]{3,1,2,0:T(8,128)(2,1)S(1)}, bf16[2,64,2,128]{3,1,2,0:T(8,128)(2,1)S(1)}, u32[]{:S(2)}, u32[]{:S(2)}) %collective-permute-start.5) | collective-permute-done | bytes 65568 | tf_op jit(solution)/shard_map/ppermute | solution.py:24
  17.8 0.0 collective-permute-done.6
  17.9 0.0 copy-done
  17.9 0.8 %fusion.16 = (f32[2,8,64]{2,1,0:T(8,128)S(1)}, bf16[2,8,64,512]{3,2,1,0:T(8,128)(2,1)S(1)}) fusion(pred[64,512]{1,0:T(8,128)(4,1)S(1)} %broadcast_compare_fusion, bf16[64,2,8,128]{3,2,1,0:T(8,128)(2,1)S(1)} %bitcast.34, bf16[2,512,2,128]{3,1,2,0:T(8,128)(2,1)S(1)} %constant_dynamic-update-slice_fusion), kind=kOutput, calls=%fused_computation.35 | convolution fusion | flops 136839680 | bytes 1609728 | tf_op jit(solution)/shard_map/sub | solution.py:37
  18.7 0.1 copy.12
  18.9 1.4 %fusion.3 = bf16[64,16,128]{2,1,0:T(8,128)(2,1)} fusion(bf16[2,8,64,512]{3,2,1,0:T(8,128)(2,1)S(1)} %get-tuple-element.10, bf16[2,512,2,128]{3,1,2,0:T(8,128)(2,1)S(1)} %constant_dynamic-update-slice_fusion, f32[2,8,64]{1,0,2:T(2,128)S(1)} %copy.12), kind=kOutput, calls=%fused_computation.6 | convolution fusion | flops 134479872 | bytes 1638400 | tf_op jit(solution)/shard_map/hgqk,khd->hgqd/dot_general | solution.py:39
  (13 shorter events, 0.1 us)
Async XLA Ops:
  0.0 17.9 %copy-start = (bf16[64,16,128]{2,1,0:T(8,128)(2,1)S(1)}, bf16[64,16,128]{2,1,0:T(8,128)(2,1)}, u32[]{:S(2)}) copy-start(bf16[64,16,128]{2,1,0:T(8,128)(2,1)} %param.3) | copy-start | bytes 786436
  0.9 11.2 %collective-permute-start.4 = (bf16[2,64,2,128]{3,1,2,0:T(8,128)(2,1)S(1)}, bf16[2,64,2,128]{3,1,2,0:T(8,128)(2,1)S(1)}, u32[]{:S(2)}, u32[]{:S(2)}) collective-permute-start(bf16[2,64,2,128]{3,1,2,0:T(8,128)(2,1)S(1)} %get-tuple-element.8), channel_id=1, source_target_pairs={{0,2},{2,4},{4,6},{6,8},{8,10},{10,12},{12,14},{14,0},{1,3},{3,5},... | collective-permute-start | bytes 196616 | tf_op jit(solution)/shard_map/ppermute | solution.py:24
  3.9 9.6 %collective-permute-start.3 = (bf16[2,64,2,128]{3,1,2,0:T(8,128)(2,1)S(1)}, bf16[2,64,2,128]{3,1,2,0:T(8,128)(2,1)S(1)}, u32[]{:S(2)}, u32[]{:S(2)}) collective-permute-start(bf16[2,64,2,128]{3,1,2,0:T(8,128)(2,1)S(1)} %get-tuple-element.8), channel_id=1, source_target_pairs={{0,4},{2,6},{4,8},{6,10},{8,12},{10,14},{12,0},{14,2},{1,5},{3,7},... | collective-permute-start | bytes 196616 | tf_op jit(solution)/shard_map/ppermute | solution.py:24
  5.5 11.3 %collective-permute-start.2 = (bf16[2,64,2,128]{3,1,2,0:T(8,128)(2,1)S(1)}, bf16[2,64,2,128]{3,1,2,0:T(8,128)(2,1)S(1)}, u32[]{:S(2)}, u32[]{:S(2)}) collective-permute-start(bf16[2,64,2,128]{3,1,2,0:T(8,128)(2,1)S(1)} %get-tuple-element.8), channel_id=1, source_target_pairs={{0,6},{2,8},{4,10},{6,12},{8,14},{10,0},{12,2},{14,4},{1,7},{3,9},... | collective-permute-start | bytes 196616 | tf_op jit(solution)/shard_map/ppermute | solution.py:24
  8.0 8.7 %collective-permute-start.1 = (bf16[2,64,2,128]{3,1,2,0:T(8,128)(2,1)S(1)}, bf16[2,64,2,128]{3,1,2,0:T(8,128)(2,1)S(1)}, u32[]{:S(2)}, u32[]{:S(2)}) collective-permute-start(bf16[2,64,2,128]{3,1,2,0:T(8,128)(2,1)S(1)} %get-tuple-element.8), channel_id=1, source_target_pairs={{0,8},{2,10},{4,12},{6,14},{8,0},{10,2},{12,4},{14,6},{1,9},{3,11}... | collective-permute-start | bytes 196616 | tf_op jit(solution)/shard_map/ppermute | solution.py:24
  9.3 7.5 %collective-permute-start = (bf16[2,64,2,128]{3,1,2,0:T(8,128)(2,1)S(1)}, bf16[2,64,2,128]{3,1,2,0:T(8,128)(2,1)S(1)}, u32[]{:S(2)}, u32[]{:S(2)}) collective-permute-start(bf16[2,64,2,128]{3,1,2,0:T(8,128)(2,1)S(1)} %get-tuple-element.8), channel_id=1, source_target_pairs={{0,10},{2,12},{4,14},{6,0},{8,2},{10,4},{12,6},{14,8},{1,11},{3,13... | collective-permute-start | bytes 196616 | tf_op jit(solution)/shard_map/ppermute | solution.py:24
  12.1 5.7 %collective-permute-start.5 = (bf16[2,64,2,128]{3,1,2,0:T(8,128)(2,1)S(1)}, bf16[2,64,2,128]{3,1,2,0:T(8,128)(2,1)S(1)}, u32[]{:S(2)}, u32[]{:S(2)}) collective-permute-start(bf16[2,64,2,128]{3,1,2,0:T(8,128)(2,1)S(1)} %get-tuple-element.8), channel_id=1, source_target_pairs={{0,12},{2,14},{4,0},{6,2},{8,4},{10,6},{12,8},{14,10},{1,13},{3,15... | collective-permute-start | bytes 196616 | tf_op jit(solution)/shard_map/ppermute | solution.py:24
  13.5 4.3 %collective-permute-start.6 = (bf16[2,64,2,128]{3,1,2,0:T(8,128)(2,1)S(1)}, bf16[2,64,2,128]{3,1,2,0:T(8,128)(2,1)S(1)}, u32[]{:S(2)}, u32[]{:S(2)}) collective-permute-start(bf16[2,64,2,128]{3,1,2,0:T(8,128)(2,1)S(1)} %get-tuple-element.8), channel_id=1, source_target_pairs={{0,14},{2,0},{4,2},{6,4},{8,6},{10,8},{12,10},{14,12},{1,15},{3,1}... | collective-permute-start | bytes 196616 | tf_op jit(solution)/shard_map/ppermute | solution.py:24

commit v7 on v4

--- a/solution.py
+++ b/solution.py
@@ -32,7 +32,7 @@
     rows = queries.reshape(local_rows, key_heads, group_size, head_size)
     scores = jnp.einsum("qhgd,khd->hgqk", rows, key_all, preferred_element_type=jnp.float32) * scale
     valid = key_position[None, :] <= position[:, None]
-    scores = jnp.where(valid, scores, -1e30)
+    scores = lax.optimization_barrier(jnp.where(valid, scores, -1e30))
     row_max = jnp.max(scores, axis=-1)
     weights = jnp.exp(scores - row_max[..., None])
     total = jnp.sum(weights, axis=-1)

time: 20.4 us -> 20.6 us (level)
  other arithmetic: 0.13 us -> 0.67 us
  matrix products: 2.29 us -> 1.9 us
    sub x1 -> x0, matrix products: 0.84 us -> none  [per_device(): weights = jnp.exp(scores - row_max[..., None])]
    sub x0 -> x1, other arithmetic: none -> 0.53 us  [per_device(): weights = jnp.exp(scores - row_max[..., None])]
    dot_general x0 -> x1, matrix products: none -> 0.45 us  [per_device(): jnp.einsum('qhgd,khd->hgqk', rows, key_all, preferred_element_type=jnp.fl...]
where the time goes in v7:
time: 20.6 us; the launch traced here: 20.4 us
  starting transfers between devices  13.8 us (67%)
  waiting for transfers between devices  2.79 us (14%)
  matrix products  1.9 us (9%)
  local copies, waits for them, and re-layouts  1.11 us (5%)
  other arithmetic  0.67 us (3%)
    ppermute x7, starting transfers between devices, per_device(): lax.ppermute(operand, 'ctx', [(i, (i + shift) % context_size) for i in ra...  13.8 us
    ppermute x7, waiting for transfers between devices, per_device(): lax.ppermute(operand, 'ctx', [(i, (i + shift) % context_size) for i in ra...  2.79 us
    dot_general x1, matrix products, per_device(): jnp.einsum('hgqk,khd->hgqd', weights.astype(jnp.bfloat16), value_all, pre...  1.45 us
    another operation x1, local copies, waits for them, and re-layouts, per_device(): pair = jnp.stack([keys, values], axis=0)  0.83 us
    sub x1, other arithmetic, per_device(): weights = jnp.exp(scores - row_max[..., None])  0.53 us
    dot_general x1, matrix products, per_device(): jnp.einsum('qhgd,khd->hgqk', rows, key_all, preferred_element_type=jnp.fl...  0.45 us
  transfers between devices with their start and end apart: 7, of which 2 were waited for; matrix products, arithmetic and copies ran while one was open for 1% of the time, Pallas kernels for 0%

profile of v7, /device:TPU:0, one launch (start us, length us, event | category | flops | bytes accessed | tf_op | source)
XLA Modules:
  0.0 20.4 jit_solution(4409989041986061746)
XLA Ops:
  0.0 0.0 copy-start
  0.0 0.8 %copy_bitcast_fusion = (bf16[1,64,2,128]{3,1,2,0:T(8,128)(2,1)S(1)}, bf16[1,64,2,128]{3,1,2,0:T(8,128)(2,1)S(1)}) fusion(bf16[64,2,128]{2,1,0:T(2,128)(2,1)} %param.5, bf16[64,2,128]{2,1,0:T(2,128)(2,1)} %param.4), kind=kLoop, calls=%fused_computation.12 | loop fusion | bytes 131072 | tf_op jit(solution)/shard_map/stack | solution.py:17
  0.9 3.0 %collective-permute-start.4 = (bf16[2,64,2,128]{3,1,2,0:T(8,128)(2,1)S(1)}, bf16[2,64,2,128]{3,1,2,0:T(8,128)(2,1)S(1)}, u32[]{:S(2)}, u32[]{:S(2)}) collective-permute-start(bf16[2,64,2,128]{3,1,2,0:T(8,128)(2,1)S(1)} %get-tuple-element.8), channel_id=1, source_target_pairs={{0,2},{2,4},{4,6},{6,8},{8,10},{10,12},{12,14},{14,0},{1,3},{3,5},... | collective-permute-start | bytes 196616 | tf_op jit(solution)/shard_map/ppermute | solution.py:24
  3.9 1.6 %collective-permute-start.3 = (bf16[2,64,2,128]{3,1,2,0:T(8,128)(2,1)S(1)}, bf16[2,64,2,128]{3,1,2,0:T(8,128)(2,1)S(1)}, u32[]{:S(2)}, u32[]{:S(2)}) collective-permute-start(bf16[2,64,2,128]{3,1,2,0:T(8,128)(2,1)S(1)} %get-tuple-element.8), channel_id=1, source_target_pairs={{0,4},{2,6},{4,8},{6,10},{8,12},{10,14},{12,0},{14,2},{1,5},{3,7},... | collective-permute-start | bytes 196616 | tf_op jit(solution)/shard_map/ppermute | solution.py:24
  5.5 2.6 %collective-permute-start.2 = (bf16[2,64,2,128]{3,1,2,0:T(8,128)(2,1)S(1)}, bf16[2,64,2,128]{3,1,2,0:T(8,128)(2,1)S(1)}, u32[]{:S(2)}, u32[]{:S(2)}) collective-permute-start(bf16[2,64,2,128]{3,1,2,0:T(8,128)(2,1)S(1)} %get-tuple-element.8), channel_id=1, source_target_pairs={{0,6},{2,8},{4,10},{6,12},{8,14},{10,0},{12,2},{14,4},{1,7},{3,9},... | collective-permute-start | bytes 196616 | tf_op jit(solution)/shard_map/ppermute | solution.py:24
  8.0 1.2 %collective-permute-start.1 = (bf16[2,64,2,128]{3,1,2,0:T(8,128)(2,1)S(1)}, bf16[2,64,2,128]{3,1,2,0:T(8,128)(2,1)S(1)}, u32[]{:S(2)}, u32[]{:S(2)}) collective-permute-start(bf16[2,64,2,128]{3,1,2,0:T(8,128)(2,1)S(1)} %get-tuple-element.8), channel_id=1, source_target_pairs={{0,8},{2,10},{4,12},{6,14},{8,0},{10,2},{12,4},{14,6},{1,9},{3,11}... | collective-permute-start | bytes 196616 | tf_op jit(solution)/shard_map/ppermute | solution.py:24
  9.3 2.6 %collective-permute-start = (bf16[2,64,2,128]{3,1,2,0:T(8,128)(2,1)S(1)}, bf16[2,64,2,128]{3,1,2,0:T(8,128)(2,1)S(1)}, u32[]{:S(2)}, u32[]{:S(2)}) collective-permute-start(bf16[2,64,2,128]{3,1,2,0:T(8,128)(2,1)S(1)} %get-tuple-element.8), channel_id=1, source_target_pairs={{0,10},{2,12},{4,14},{6,0},{8,2},{10,4},{12,6},{14,8},{1,11},{3,13... | collective-permute-start | bytes 196616 | tf_op jit(solution)/shard_map/ppermute | solution.py:24
  11.9 0.1 concatenate.6
  12.0 0.1 broadcast_compare_fusion
  12.1 0.0 collective-permute-done.4
  12.1 1.4 %collective-permute-start.5 = (bf16[2,64,2,128]{3,1,2,0:T(8,128)(2,1)S(1)}, bf16[2,64,2,128]{3,1,2,0:T(8,128)(2,1)S(1)}, u32[]{:S(2)}, u32[]{:S(2)}) collective-permute-start(bf16[2,64,2,128]{3,1,2,0:T(8,128)(2,1)S(1)} %get-tuple-element.8), channel_id=1, source_target_pairs={{0,12},{2,14},{4,0},{6,2},{8,4},{10,6},{12,8},{14,10},{1,13},{3,15... | collective-permute-start | bytes 196616 | tf_op jit(solution)/shard_map/ppermute | solution.py:24
  13.5 0.0 collective-permute-done.3
  13.5 1.4 %collective-permute-start.6 = (bf16[2,64,2,128]{3,1,2,0:T(8,128)(2,1)S(1)}, bf16[2,64,2,128]{3,1,2,0:T(8,128)(2,1)S(1)}, u32[]{:S(2)}, u32[]{:S(2)}) collective-permute-start(bf16[2,64,2,128]{3,1,2,0:T(8,128)(2,1)S(1)} %get-tuple-element.8), channel_id=1, source_target_pairs={{0,14},{2,0},{4,2},{6,4},{8,6},{10,8},{12,10},{14,12},{1,15},{3,1}... | collective-permute-start | bytes 196616 | tf_op jit(solution)/shard_map/ppermute | solution.py:24
  14.9 1.8 %collective-permute-done = bf16[2,64,2,128]{3,1,2,0:T(8,128)(2,1)S(1)} collective-permute-done((bf16[2,64,2,128]{3,1,2,0:T(8,128)(2,1)S(1)}, bf16[2,64,2,128]{3,1,2,0:T(8,128)(2,1)S(1)}, u32[]{:S(2)}, u32[]{:S(2)}) %collective-permute-start) | collective-permute-done | bytes 65568 | tf_op jit(solution)/shard_map/ppermute | solution.py:24
  16.8 0.0 collective-permute-done.1
  16.8 0.0 collective-permute-done.2
  16.9 1.0 %collective-permute-done.5 = bf16[2,64,2,128]{3,1,2,0:T(8,128)(2,1)S(1)} collective-permute-done((bf16[2,64,2,128]{3,1,2,0:T(8,128)(2,1)S(1)}, bf16[2,64,2,128]{3,1,2,0:T(8,128)(2,1)S(1)}, u32[]{:S(2)}, u32[]{:S(2)}) %collective-permute-start.5) | collective-permute-done | bytes 65568 | tf_op jit(solution)/shard_map/ppermute | solution.py:24
  17.8 0.0 collective-permute-done.6
  17.9 0.0 copy-done
  17.9 0.5 %bitcast_select_fusion = f32[2,8,64,512]{3,2,1,0:T(8,128)S(1)} fusion(pred[64,512]{1,0:T(8,128)(4,1)S(1)} %broadcast_compare_fusion, bf16[2,512,2,128]{3,1,2,0:T(8,128)(2,1)S(1)} %constant_dynamic-update-slice_fusion, bf16[64,2,8,128]{3,2,1,0:T(8,128)(2,1)S(1)} %bitcast.22), kind=kOutput, calls=%fused_computation.1 | convolution fusion | flops 135266304 | bytes 2654208 | tf_op jit(solution)/shard_map/qhgd,khd->hgqk/dot_general | solution.py:33
  18.3 0.5 %fusion.5 = (f32[2,8,64]{2,1,0:T(8,128)S(1)}, bf16[2,8,64,512]{3,2,1,0:T(8,128)(2,1)S(1)}) fusion(f32[2,8,64,512]{3,2,1,0:T(8,128)S(1)} %bitcast_select_fusion), kind=kOutput, calls=%fused_computation.30 | output fusion | flops 1573375 | bytes 3149824 | tf_op jit(solution)/shard_map/sub | solution.py:37
  18.9 0.1 copy.12
  19.0 1.4 %fusion.2 = bf16[64,16,128]{2,1,0:T(8,128)(2,1)} fusion(bf16[2,8,64,512]{3,2,1,0:T(8,128)(2,1)S(1)} %get-tuple-element.10, bf16[2,512,2,128]{3,1,2,0:T(8,128)(2,1)S(1)} %constant_dynamic-update-slice_fusion, f32[2,8,64]{1,0,2:T(2,128)S(1)} %copy.12), kind=kOutput, calls=%fused_computation.5 | convolution fusion | flops 134479872 | bytes 1638400 | tf_op jit(solution)/shard_map/hgqk,khd->hgqd/dot_general | solution.py:39
  (13 shorter events, 0.1 us)
Async XLA Ops:
  0.0 17.9 %copy-start = (bf16[64,16,128]{2,1,0:T(8,128)(2,1)S(1)}, bf16[64,16,128]{2,1,0:T(8,128)(2,1)}, u32[]{:S(2)}) copy-start(bf16[64,16,128]{2,1,0:T(8,128)(2,1)} %param.3) | copy-start | bytes 786436
  0.9 11.2 %collective-permute-start.4 = (bf16[2,64,2,128]{3,1,2,0:T(8,128)(2,1)S(1)}, bf16[2,64,2,128]{3,1,2,0:T(8,128)(2,1)S(1)}, u32[]{:S(2)}, u32[]{:S(2)}) collective-permute-start(bf16[2,64,2,128]{3,1,2,0:T(8,128)(2,1)S(1)} %get-tuple-element.8), channel_id=1, source_target_pairs={{0,2},{2,4},{4,6},{6,8},{8,10},{10,12},{12,14},{14,0},{1,3},{3,5},... | collective-permute-start | bytes 196616 | tf_op jit(solution)/shard_map/ppermute | solution.py:24
  3.9 9.6 %collective-permute-start.3 = (bf16[2,64,2,128]{3,1,2,0:T(8,128)(2,1)S(1)}, bf16[2,64,2,128]{3,1,2,0:T(8,128)(2,1)S(1)}, u32[]{:S(2)}, u32[]{:S(2)}) collective-permute-start(bf16[2,64,2,128]{3,1,2,0:T(8,128)(2,1)S(1)} %get-tuple-element.8), channel_id=1, source_target_pairs={{0,4},{2,6},{4,8},{6,10},{8,12},{10,14},{12,0},{14,2},{1,5},{3,7},... | collective-permute-start | bytes 196616 | tf_op jit(solution)/shard_map/ppermute | solution.py:24
  5.5 11.3 %collective-permute-start.2 = (bf16[2,64,2,128]{3,1,2,0:T(8,128)(2,1)S(1)}, bf16[2,64,2,128]{3,1,2,0:T(8,128)(2,1)S(1)}, u32[]{:S(2)}, u32[]{:S(2)}) collective-permute-start(bf16[2,64,2,128]{3,1,2,0:T(8,128)(2,1)S(1)} %get-tuple-element.8), channel_id=1, source_target_pairs={{0,6},{2,8},{4,10},{6,12},{8,14},{10,0},{12,2},{14,4},{1,7},{3,9},... | collective-permute-start | bytes 196616 | tf_op jit(solution)/shard_map/ppermute | solution.py:24
  8.0 8.7 %collective-permute-start.1 = (bf16[2,64,2,128]{3,1,2,0:T(8,128)(2,1)S(1)}, bf16[2,64,2,128]{3,1,2,0:T(8,128)(2,1)S(1)}, u32[]{:S(2)}, u32[]{:S(2)}) collective-permute-start(bf16[2,64,2,128]{3,1,2,0:T(8,128)(2,1)S(1)} %get-tuple-element.8), channel_id=1, source_target_pairs={{0,8},{2,10},{4,12},{6,14},{8,0},{10,2},{12,4},{14,6},{1,9},{3,11}... | collective-permute-start | bytes 196616 | tf_op jit(solution)/shard_map/ppermute | solution.py:24
  9.3 7.5 %collective-permute-start = (bf16[2,64,2,128]{3,1,2,0:T(8,128)(2,1)S(1)}, bf16[2,64,2,128]{3,1,2,0:T(8,128)(2,1)S(1)}, u32[]{:S(2)}, u32[]{:S(2)}) collective-permute-start(bf16[2,64,2,128]{3,1,2,0:T(8,128)(2,1)S(1)} %get-tuple-element.8), channel_id=1, source_target_pairs={{0,10},{2,12},{4,14},{6,0},{8,2},{10,4},{12,6},{14,8},{1,11},{3,13... | collective-permute-start | bytes 196616 | tf_op jit(solution)/shard_map/ppermute | solution.py:24
  12.1 5.7 %collective-permute-start.5 = (bf16[2,64,2,128]{3,1,2,0:T(8,128)(2,1)S(1)}, bf16[2,64,2,128]{3,1,2,0:T(8,128)(2,1)S(1)}, u32[]{:S(2)}, u32[]{:S(2)}) collective-permute-start(bf16[2,64,2,128]{3,1,2,0:T(8,128)(2,1)S(1)} %get-tuple-element.8), channel_id=1, source_target_pairs={{0,12},{2,14},{4,0},{6,2},{8,4},{10,6},{12,8},{14,10},{1,13},{3,15... | collective-permute-start | bytes 196616 | tf_op jit(solution)/shard_map/ppermute | solution.py:24
  13.5 4.3 %collective-permute-start.6 = (bf16[2,64,2,128]{3,1,2,0:T(8,128)(2,1)S(1)}, bf16[2,64,2,128]{3,1,2,0:T(8,128)(2,1)S(1)}, u32[]{:S(2)}, u32[]{:S(2)}) collective-permute-start(bf16[2,64,2,128]{3,1,2,0:T(8,128)(2,1)S(1)} %get-tuple-element.8), channel_id=1, source_target_pairs={{0,14},{2,0},{4,2},{6,4},{8,6},{10,8},{12,10},{14,12},{1,15},{3,1}... | collective-permute-start | bytes 196616 | tf_op jit(solution)/shard_map/ppermute | solution.py:24

commit v8 on v4

--- a/solution.py
+++ b/solution.py
@@ -16,13 +16,13 @@
     position = me * local_rows + offset
     pair = jnp.stack([keys, values], axis=0)
     moved = {}
-    after = {6: 1, 7: 2} if context_size == 8 else {}
+    after = {7: 1, 6: 2} if context_size == 8 else {}
     for shift in range(1, context_size):
         operand = pair
         if shift in after:
             operand = lax.optimization_barrier((pair, moved[after[shift]]))[0]
         moved[shift] = lax.ppermute(operand, "ctx", [(i, (i + shift) % context_size) for i in range(context_size)])
-    order = [5, 4, 3, 2, 1, 6, 7] if context_size == 8 else list(range(1, context_size))
+    order = [5, 4, 3, 2, 1, 7, 6] if context_size == 8 else list(range(1, context_size))
     pieces = [pair] + [moved[shift] for shift in order]
     sources = [me * local_rows + offset] + [((me - shift) % context_size) * local_rows + offset for shift in order]
     gathered = jnp.concatenate(pieces, axis=1)

time: 20.4 us -> 21.1 us (1.034)
  waiting for transfers between devices: 2.79 us -> 3.46 us
    ppermute x7, waiting for transfers between devices: 2.79 us -> 3.46 us  [per_device(): lax.ppermute(operand, 'ctx', [(i, (i + shift) % context_size) for i in ra...]
where the time goes in v8:
time: 21.1 us; the launch traced here: 21 us
  starting transfers between devices  13.8 us (65%)
  waiting for transfers between devices  3.46 us (16%)
  matrix products  2.29 us (11%)
  local copies, waits for them, and re-layouts  1.12 us (5%)
    ppermute x7, starting transfers between devices, per_device(): lax.ppermute(operand, 'ctx', [(i, (i + shift) % context_size) for i in ra...  13.8 us
    ppermute x7, waiting for transfers between devices, per_device(): lax.ppermute(operand, 'ctx', [(i, (i + shift) % context_size) for i in ra...  3.46 us
    dot_general x1, matrix products, per_device(): jnp.einsum('hgqk,khd->hgqd', weights.astype(jnp.bfloat16), value_all, pre...  1.45 us
    sub x1, matrix products, per_device(): weights = jnp.exp(scores - row_max[..., None])  0.84 us
    another operation x1, local copies, waits for them, and re-layouts, per_device(): pair = jnp.stack([keys, values], axis=0)  0.83 us
  transfers between devices with their start and end apart: 7, of which 2 were waited for; matrix products, arithmetic and copies ran while one was open for 1% of the time, Pallas kernels for 0%

profile of v8, /device:TPU:0, one launch (start us, length us, event | category | flops | bytes accessed | tf_op | source)
XLA Modules:
  0.0 21.0 jit_solution(6387006363971040618)
XLA Ops:
  0.0 0.0 copy-start
  0.0 0.8 %copy_bitcast_fusion = (bf16[1,64,2,128]{3,1,2,0:T(8,128)(2,1)S(1)}, bf16[1,64,2,128]{3,1,2,0:T(8,128)(2,1)S(1)}) fusion(bf16[64,2,128]{2,1,0:T(2,128)(2,1)} %param.5, bf16[64,2,128]{2,1,0:T(2,128)(2,1)} %param.4), kind=kLoop, calls=%fused_computation.17 | loop fusion | bytes 131072 | tf_op jit(solution)/shard_map/stack | solution.py:17
  0.9 3.0 %collective-permute-start.4 = (bf16[2,64,2,128]{3,1,2,0:T(8,128)(2,1)S(1)}, bf16[2,64,2,128]{3,1,2,0:T(8,128)(2,1)S(1)}, u32[]{:S(2)}, u32[]{:S(2)}) collective-permute-start(bf16[2,64,2,128]{3,1,2,0:T(8,128)(2,1)S(1)} %get-tuple-element.8), channel_id=1, source_target_pairs={{0,2},{2,4},{4,6},{6,8},{8,10},{10,12},{12,14},{14,0},{1,3},{3,5},... | collective-permute-start | bytes 196616 | tf_op jit(solution)/shard_map/ppermute | solution.py:24
  3.9 1.6 %collective-permute-start.3 = (bf16[2,64,2,128]{3,1,2,0:T(8,128)(2,1)S(1)}, bf16[2,64,2,128]{3,1,2,0:T(8,128)(2,1)S(1)}, u32[]{:S(2)}, u32[]{:S(2)}) collective-permute-start(bf16[2,64,2,128]{3,1,2,0:T(8,128)(2,1)S(1)} %get-tuple-element.8), channel_id=1, source_target_pairs={{0,4},{2,6},{4,8},{6,10},{8,12},{10,14},{12,0},{14,2},{1,5},{3,7},... | collective-permute-start | bytes 196616 | tf_op jit(solution)/shard_map/ppermute | solution.py:24
  5.5 2.6 %collective-permute-start.2 = (bf16[2,64,2,128]{3,1,2,0:T(8,128)(2,1)S(1)}, bf16[2,64,2,128]{3,1,2,0:T(8,128)(2,1)S(1)}, u32[]{:S(2)}, u32[]{:S(2)}) collective-permute-start(bf16[2,64,2,128]{3,1,2,0:T(8,128)(2,1)S(1)} %get-tuple-element.8), channel_id=1, source_target_pairs={{0,6},{2,8},{4,10},{6,12},{8,14},{10,0},{12,2},{14,4},{1,7},{3,9},... | collective-permute-start | bytes 196616 | tf_op jit(solution)/shard_map/ppermute | solution.py:24
  8.0 1.2 %collective-permute-start.1 = (bf16[2,64,2,128]{3,1,2,0:T(8,128)(2,1)S(1)}, bf16[2,64,2,128]{3,1,2,0:T(8,128)(2,1)S(1)}, u32[]{:S(2)}, u32[]{:S(2)}) collective-permute-start(bf16[2,64,2,128]{3,1,2,0:T(8,128)(2,1)S(1)} %get-tuple-element.8), channel_id=1, source_target_pairs={{0,8},{2,10},{4,12},{6,14},{8,0},{10,2},{12,4},{14,6},{1,9},{3,11}... | collective-permute-start | bytes 196616 | tf_op jit(solution)/shard_map/ppermute | solution.py:24
  9.3 2.6 %collective-permute-start = (bf16[2,64,2,128]{3,1,2,0:T(8,128)(2,1)S(1)}, bf16[2,64,2,128]{3,1,2,0:T(8,128)(2,1)S(1)}, u32[]{:S(2)}, u32[]{:S(2)}) collective-permute-start(bf16[2,64,2,128]{3,1,2,0:T(8,128)(2,1)S(1)} %get-tuple-element.8), channel_id=1, source_target_pairs={{0,10},{2,12},{4,14},{6,0},{8,2},{10,4},{12,6},{14,8},{1,11},{3,13... | collective-permute-start | bytes 196616 | tf_op jit(solution)/shard_map/ppermute | solution.py:24
  11.9 0.1 concatenate.6
  12.0 0.1 broadcast_compare_fusion
  12.1 0.0 collective-permute-done.4
  12.1 1.5 %collective-permute-start.5 = (bf16[2,64,2,128]{3,1,2,0:T(8,128)(2,1)S(1)}, bf16[2,64,2,128]{3,1,2,0:T(8,128)(2,1)S(1)}, u32[]{:S(2)}, u32[]{:S(2)}) collective-permute-start(bf16[2,64,2,128]{3,1,2,0:T(8,128)(2,1)S(1)} %get-tuple-element.8), channel_id=1, source_target_pairs={{0,14},{2,0},{4,2},{6,4},{8,6},{10,8},{12,10},{14,12},{1,15},{3,1}... | collective-permute-start | bytes 196616 | tf_op jit(solution)/shard_map/ppermute | solution.py:24
  13.6 0.0 collective-permute-done.3
  13.6 1.3 %collective-permute-start.6 = (bf16[2,64,2,128]{3,1,2,0:T(8,128)(2,1)S(1)}, bf16[2,64,2,128]{3,1,2,0:T(8,128)(2,1)S(1)}, u32[]{:S(2)}, u32[]{:S(2)}) collective-permute-start(bf16[2,64,2,128]{3,1,2,0:T(8,128)(2,1)S(1)} %get-tuple-element.8), channel_id=1, source_target_pairs={{0,12},{2,14},{4,0},{6,2},{8,4},{10,6},{12,8},{14,10},{1,13},{3,15... | collective-permute-start | bytes 196616 | tf_op jit(solution)/shard_map/ppermute | solution.py:24
  14.9 1.8 %collective-permute-done = bf16[2,64,2,128]{3,1,2,0:T(8,128)(2,1)S(1)} collective-permute-done((bf16[2,64,2,128]{3,1,2,0:T(8,128)(2,1)S(1)}, bf16[2,64,2,128]{3,1,2,0:T(8,128)(2,1)S(1)}, u32[]{:S(2)}, u32[]{:S(2)}) %collective-permute-start) | collective-permute-done | bytes 65568 | tf_op jit(solution)/shard_map/ppermute | solution.py:24
  16.8 0.0 collective-permute-done.1
  16.8 0.0 collective-permute-done.2
  16.9 0.0 collective-permute-done.5
  16.9 1.6 %collective-permute-done.6 = bf16[2,64,2,128]{3,1,2,0:T(8,128)(2,1)S(1)} collective-permute-done((bf16[2,64,2,128]{3,1,2,0:T(8,128)(2,1)S(1)}, bf16[2,64,2,128]{3,1,2,0:T(8,128)(2,1)S(1)}, u32[]{:S(2)}, u32[]{:S(2)}) %collective-permute-start.6) | collective-permute-done | bytes 65568 | tf_op jit(solution)/shard_map/ppermute | solution.py:24
  18.5 0.0 copy-done
  18.6 0.8 %fusion.18 = (f32[2,8,64]{2,1,0:T(8,128)S(1)}, bf16[2,8,64,512]{3,2,1,0:T(8,128)(2,1)S(1)}) fusion(pred[64,512]{1,0:T(8,128)(4,1)S(1)} %broadcast_compare_fusion, bf16[64,2,8,128]{3,2,1,0:T(8,128)(2,1)S(1)} %bitcast.34, bf16[2,512,2,128]{3,1,2,0:T(8,128)(2,1)S(1)} %constant_dynamic-update-slice_fusion), kind=kOutput, calls=%fused_computation.37 | convolution fusion | flops 136839680 | bytes 1609728 | tf_op jit(solution)/shard_map/sub | solution.py:37
  19.4 0.1 copy.12
  19.5 1.4 %fusion.3 = bf16[64,16,128]{2,1,0:T(8,128)(2,1)} fusion(bf16[2,8,64,512]{3,2,1,0:T(8,128)(2,1)S(1)} %get-tuple-element.10, bf16[2,512,2,128]{3,1,2,0:T(8,128)(2,1)S(1)} %constant_dynamic-update-slice_fusion, f32[2,8,64]{1,0,2:T(2,128)S(1)} %copy.12), kind=kOutput, calls=%fused_computation.6 | convolution fusion | flops 134479872 | bytes 1638400 | tf_op jit(solution)/shard_map/hgqk,khd->hgqd/dot_general | solution.py:39
  (13 shorter events, 0.1 us)
Async XLA Ops:
  0.0 18.6 %copy-start = (bf16[64,16,128]{2,1,0:T(8,128)(2,1)S(1)}, bf16[64,16,128]{2,1,0:T(8,128)(2,1)}, u32[]{:S(2)}) copy-start(bf16[64,16,128]{2,1,0:T(8,128)(2,1)} %param.3) | copy-start | bytes 786436
  0.9 11.2 %collective-permute-start.4 = (bf16[2,64,2,128]{3,1,2,0:T(8,128)(2,1)S(1)}, bf16[2,64,2,128]{3,1,2,0:T(8,128)(2,1)S(1)}, u32[]{:S(2)}, u32[]{:S(2)}) collective-permute-start(bf16[2,64,2,128]{3,1,2,0:T(8,128)(2,1)S(1)} %get-tuple-element.8), channel_id=1, source_target_pairs={{0,2},{2,4},{4,6},{6,8},{8,10},{10,12},{12,14},{14,0},{1,3},{3,5},... | collective-permute-start | bytes 196616 | tf_op jit(solution)/shard_map/ppermute | solution.py:24
  3.9 9.7 %collective-permute-start.3 = (bf16[2,64,2,128]{3,1,2,0:T(8,128)(2,1)S(1)}, bf16[2,64,2,128]{3,1,2,0:T(8,128)(2,1)S(1)}, u32[]{:S(2)}, u32[]{:S(2)}) collective-permute-start(bf16[2,64,2,128]{3,1,2,0:T(8,128)(2,1)S(1)} %get-tuple-element.8), channel_id=1, source_target_pairs={{0,4},{2,6},{4,8},{6,10},{8,12},{10,14},{12,0},{14,2},{1,5},{3,7},... | collective-permute-start | bytes 196616 | tf_op jit(solution)/shard_map/ppermute | solution.py:24
  5.5 11.3 %collective-permute-start.2 = (bf16[2,64,2,128]{3,1,2,0:T(8,128)(2,1)S(1)}, bf16[2,64,2,128]{3,1,2,0:T(8,128)(2,1)S(1)}, u32[]{:S(2)}, u32[]{:S(2)}) collective-permute-start(bf16[2,64,2,128]{3,1,2,0:T(8,128)(2,1)S(1)} %get-tuple-element.8), channel_id=1, source_target_pairs={{0,6},{2,8},{4,10},{6,12},{8,14},{10,0},{12,2},{14,4},{1,7},{3,9},... | collective-permute-start | bytes 196616 | tf_op jit(solution)/shard_map/ppermute | solution.py:24
  8.0 8.8 %collective-permute-start.1 = (bf16[2,64,2,128]{3,1,2,0:T(8,128)(2,1)S(1)}, bf16[2,64,2,128]{3,1,2,0:T(8,128)(2,1)S(1)}, u32[]{:S(2)}, u32[]{:S(2)}) collective-permute-start(bf16[2,64,2,128]{3,1,2,0:T(8,128)(2,1)S(1)} %get-tuple-element.8), channel_id=1, source_target_pairs={{0,8},{2,10},{4,12},{6,14},{8,0},{10,2},{12,4},{14,6},{1,9},{3,11}... | collective-permute-start | bytes 196616 | tf_op jit(solution)/shard_map/ppermute | solution.py:24
  9.3 7.5 %collective-permute-start = (bf16[2,64,2,128]{3,1,2,0:T(8,128)(2,1)S(1)}, bf16[2,64,2,128]{3,1,2,0:T(8,128)(2,1)S(1)}, u32[]{:S(2)}, u32[]{:S(2)}) collective-permute-start(bf16[2,64,2,128]{3,1,2,0:T(8,128)(2,1)S(1)} %get-tuple-element.8), channel_id=1, source_target_pairs={{0,10},{2,12},{4,14},{6,0},{8,2},{10,4},{12,6},{14,8},{1,11},{3,13... | collective-permute-start | bytes 196616 | tf_op jit(solution)/shard_map/ppermute | solution.py:24
  12.1 4.8 %collective-permute-start.5 = (bf16[2,64,2,128]{3,1,2,0:T(8,128)(2,1)S(1)}, bf16[2,64,2,128]{3,1,2,0:T(8,128)(2,1)S(1)}, u32[]{:S(2)}, u32[]{:S(2)}) collective-permute-start(bf16[2,64,2,128]{3,1,2,0:T(8,128)(2,1)S(1)} %get-tuple-element.8), channel_id=1, source_target_pairs={{0,14},{2,0},{4,2},{6,4},{8,6},{10,8},{12,10},{14,12},{1,15},{3,1}... | collective-permute-start | bytes 196616 | tf_op jit(solution)/shard_map/ppermute | solution.py:24
  13.6 4.9 %collective-permute-start.6 = (bf16[2,64,2,128]{3,1,2,0:T(8,128)(2,1)S(1)}, bf16[2,64,2,128]{3,1,2,0:T(8,128)(2,1)S(1)}, u32[]{:S(2)}, u32[]{:S(2)}) collective-permute-start(bf16[2,64,2,128]{3,1,2,0:T(8,128)(2,1)S(1)} %get-tuple-element.8), channel_id=1, source_target_pairs={{0,12},{2,14},{4,0},{6,2},{8,4},{10,6},{12,8},{14,10},{1,13},{3,15... | collective-permute-start | bytes 196616 | tf_op jit(solution)/shard_map/ppermute | solution.py:24

commit v9 on v4

--- a/solution.py
+++ b/solution.py
@@ -16,15 +16,25 @@
     position = me * local_rows + offset
     pair = jnp.stack([keys, values], axis=0)
     moved = {}
+    steps = {1: (0, 1), 2: (1, 0), 3: (1, 1), 4: (2, 0), 5: (2, 1), 6: (3, 0), 7: (3, 1)}
     after = {6: 1, 7: 2} if context_size == 8 else {}
     for shift in range(1, context_size):
         operand = pair
         if shift in after:
             operand = lax.optimization_barrier((pair, moved[after[shift]]))[0]
-        moved[shift] = lax.ppermute(operand, "ctx", [(i, (i + shift) % context_size) for i in range(context_size)])
+        pairs = [(i, (i + shift) % context_size) for i in range(context_size)]
+        if context_size == 8:
+            move, flip = steps[shift]
+            pairs = [(i, 2 * ((i // 2 + move) % 4) + (i % 2 ^ flip)) for i in range(context_size)]
+        moved[shift] = lax.ppermute(operand, "ctx", pairs)
     order = [5, 4, 3, 2, 1, 6, 7] if context_size == 8 else list(range(1, context_size))
     pieces = [pair] + [moved[shift] for shift in order]
-    sources = [me * local_rows + offset] + [((me - shift) % context_size) * local_rows + offset for shift in order]
+    def source(shift):
+        if context_size == 8:
+            move, flip = steps[shift]
+            return 2 * ((me // 2 - move) % 4) + (me % 2 ^ flip)
+        return (me - shift) % context_size
+    sources = [me * local_rows + offset] + [source(shift) * local_rows + offset for shift in order]
     gathered = jnp.concatenate(pieces, axis=1)
     key_position = jnp.concatenate(sources, axis=0)
     key_all = gathered[0]

time: 20.4 us -> 21.1 us (1.034)
  waiting for transfers between devices: 2.79 us -> 4.8 us
  starting transfers between devices: 13.8 us -> 12.5 us
    ppermute x7, waiting for transfers between devices: 2.79 us -> 4.8 us  [per_device(): moved[shift] = lax.ppermute(operand, 'ctx', pairs)]
    ppermute x7, starting transfers between devices: 13.8 us -> 12.5 us  [per_device(): moved[shift] = lax.ppermute(operand, 'ctx', pairs)]
where the time goes in v9:
time: 21.1 us; the launch traced here: 21 us
  starting transfers between devices  12.5 us (59%)
  waiting for transfers between devices  4.8 us (23%)
  matrix products  2.29 us (11%)
  local copies, waits for them, and re-layouts  1.12 us (5%)
    ppermute x7, starting transfers between devices, per_device(): moved[shift] = lax.ppermute(operand, 'ctx', pairs)  12.5 us
    ppermute x7, waiting for transfers between devices, per_device(): moved[shift] = lax.ppermute(operand, 'ctx', pairs)  4.8 us
    dot_general x1, matrix products, per_device(): jnp.einsum('hgqk,khd->hgqd', weights.astype(jnp.bfloat16), value_all, pre...  1.45 us
    sub x1, matrix products, per_device(): weights = jnp.exp(scores - row_max[..., None])  0.84 us
    another operation x1, local copies, waits for them, and re-layouts, per_device(): pair = jnp.stack([keys, values], axis=0)  0.83 us
  transfers between devices with their start and end apart: 7, of which 2 were waited for; matrix products, arithmetic and copies ran while one was open for 1% of the time, Pallas kernels for 0%

profile of v9, /device:TPU:0, one launch (start us, length us, event | category | flops | bytes accessed | tf_op | source)
XLA Modules:
  0.0 21.0 jit_solution(1955613045027073202)
XLA Ops:
  0.0 0.0 copy-start
  0.0 0.8 %copy_bitcast_fusion = (bf16[1,64,2,128]{3,1,2,0:T(8,128)(2,1)S(1)}, bf16[1,64,2,128]{3,1,2,0:T(8,128)(2,1)S(1)}) fusion(bf16[64,2,128]{2,1,0:T(2,128)(2,1)} %param.5, bf16[64,2,128]{2,1,0:T(2,128)(2,1)} %param.4), kind=kLoop, calls=%fused_computation.17 | loop fusion | bytes 131072 | tf_op jit(solution)/shard_map/stack | solution.py:17
  0.9 3.0 %collective-permute-start.4 = (bf16[2,64,2,128]{3,1,2,0:T(8,128)(2,1)S(1)}, bf16[2,64,2,128]{3,1,2,0:T(8,128)(2,1)S(1)}, u32[]{:S(2)}, u32[]{:S(2)}) collective-permute-start(bf16[2,64,2,128]{3,1,2,0:T(8,128)(2,1)S(1)} %get-tuple-element.8), channel_id=1, source_target_pairs={{0,2},{2,0},{4,6},{6,4},{8,10},{10,8},{12,14},{14,12},{1,3},{3,1},... | collective-permute-start | bytes 196616 | tf_op jit(solution)/shard_map/ppermute | solution.py:29
  3.9 1.6 %collective-permute-start.3 = (bf16[2,64,2,128]{3,1,2,0:T(8,128)(2,1)S(1)}, bf16[2,64,2,128]{3,1,2,0:T(8,128)(2,1)S(1)}, u32[]{:S(2)}, u32[]{:S(2)}) collective-permute-start(bf16[2,64,2,128]{3,1,2,0:T(8,128)(2,1)S(1)} %get-tuple-element.8), channel_id=1, source_target_pairs={{0,4},{2,6},{4,8},{6,10},{8,12},{10,14},{12,0},{14,2},{1,5},{3,7},... | collective-permute-start | bytes 196616 | tf_op jit(solution)/shard_map/ppermute | solution.py:29
  5.5 1.5 %collective-permute-start.2 = (bf16[2,64,2,128]{3,1,2,0:T(8,128)(2,1)S(1)}, bf16[2,64,2,128]{3,1,2,0:T(8,128)(2,1)S(1)}, u32[]{:S(2)}, u32[]{:S(2)}) collective-permute-start(bf16[2,64,2,128]{3,1,2,0:T(8,128)(2,1)S(1)} %get-tuple-element.8), channel_id=1, source_target_pairs={{0,6},{2,4},{4,10},{6,8},{8,14},{10,12},{12,2},{14,0},{1,7},{3,5},... | collective-permute-start | bytes 196616 | tf_op jit(solution)/shard_map/ppermute | solution.py:29
  7.0 1.0 %collective-permute-start.1 = (bf16[2,64,2,128]{3,1,2,0:T(8,128)(2,1)S(1)}, bf16[2,64,2,128]{3,1,2,0:T(8,128)(2,1)S(1)}, u32[]{:S(2)}, u32[]{:S(2)}) collective-permute-start(bf16[2,64,2,128]{3,1,2,0:T(8,128)(2,1)S(1)} %get-tuple-element.8), channel_id=1, source_target_pairs={{0,8},{2,10},{4,12},{6,14},{8,0},{10,2},{12,4},{14,6},{1,9},{3,11}... | collective-permute-start | bytes 196616 | tf_op jit(solution)/shard_map/ppermute | solution.py:29
  8.1 2.8 %collective-permute-start = (bf16[2,64,2,128]{3,1,2,0:T(8,128)(2,1)S(1)}, bf16[2,64,2,128]{3,1,2,0:T(8,128)(2,1)S(1)}, u32[]{:S(2)}, u32[]{:S(2)}) collective-permute-start(bf16[2,64,2,128]{3,1,2,0:T(8,128)(2,1)S(1)} %get-tuple-element.8), channel_id=1, source_target_pairs={{0,10},{2,8},{4,14},{6,12},{8,2},{10,0},{12,6},{14,4},{1,11},{3,9}... | collective-permute-start | bytes 196616 | tf_op jit(solution)/shard_map/ppermute | solution.py:29
  10.9 0.1 concatenate.6
  11.0 0.1 broadcast_compare_fusion
  11.1 0.0 collective-permute-done.4
  11.1 2.3 %collective-permute-start.5 = (bf16[2,64,2,128]{3,1,2,0:T(8,128)(2,1)S(1)}, bf16[2,64,2,128]{3,1,2,0:T(8,128)(2,1)S(1)}, u32[]{:S(2)}, u32[]{:S(2)}) collective-permute-start(bf16[2,64,2,128]{3,1,2,0:T(8,128)(2,1)S(1)} %get-tuple-element.8), channel_id=1, source_target_pairs={{0,12},{2,14},{4,0},{6,2},{8,4},{10,6},{12,8},{14,10},{1,13},{3,15... | collective-permute-start | bytes 196616 | tf_op jit(solution)/shard_map/ppermute | solution.py:29
  13.4 0.0 collective-permute-done.3
  13.4 0.2 %collective-permute-start.6 = (bf16[2,64,2,128]{3,1,2,0:T(8,128)(2,1)S(1)}, bf16[2,64,2,128]{3,1,2,0:T(8,128)(2,1)S(1)}, u32[]{:S(2)}, u32[]{:S(2)}) collective-permute-start(bf16[2,64,2,128]{3,1,2,0:T(8,128)(2,1)S(1)} %get-tuple-element.8), channel_id=1, source_target_pairs={{0,14},{2,12},{4,2},{6,0},{8,6},{10,4},{12,10},{14,8},{1,15},{3,13... | collective-permute-start | bytes 196616 | tf_op jit(solution)/shard_map/ppermute | solution.py:29
  13.6 4.2 %collective-permute-done = bf16[2,64,2,128]{3,1,2,0:T(8,128)(2,1)S(1)} collective-permute-done((bf16[2,64,2,128]{3,1,2,0:T(8,128)(2,1)S(1)}, bf16[2,64,2,128]{3,1,2,0:T(8,128)(2,1)S(1)}, u32[]{:S(2)}, u32[]{:S(2)}) %collective-permute-start) | collective-permute-done | bytes 65568 | tf_op jit(solution)/shard_map/ppermute | solution.py:29
  17.9 0.0 collective-permute-done.1
  17.9 0.0 collective-permute-done.2
  18.0 0.0 collective-permute-done.5
  18.0 0.6 %collective-permute-done.6 = bf16[2,64,2,128]{3,1,2,0:T(8,128)(2,1)S(1)} collective-permute-done((bf16[2,64,2,128]{3,1,2,0:T(8,128)(2,1)S(1)}, bf16[2,64,2,128]{3,1,2,0:T(8,128)(2,1)S(1)}, u32[]{:S(2)}, u32[]{:S(2)}) %collective-permute-start.6) | collective-permute-done | bytes 65568 | tf_op jit(solution)/shard_map/ppermute | solution.py:29
  18.6 0.0 copy-done
  18.6 0.8 %fusion.18 = (f32[2,8,64]{2,1,0:T(8,128)S(1)}, bf16[2,8,64,512]{3,2,1,0:T(8,128)(2,1)S(1)}) fusion(pred[64,512]{1,0:T(8,128)(4,1)S(1)} %broadcast_compare_fusion, bf16[64,2,8,128]{3,2,1,0:T(8,128)(2,1)S(1)} %bitcast.34, bf16[2,512,2,128]{3,1,2,0:T(8,128)(2,1)S(1)} %constant_dynamic-update-slice_fusion), kind=kOutput, calls=%fused_computation.37 | convolution fusion | flops 136839680 | bytes 1609728 | tf_op jit(solution)/shard_map/sub | solution.py:47
  19.4 0.1 copy.12
  19.6 1.4 %fusion.3 = bf16[64,16,128]{2,1,0:T(8,128)(2,1)} fusion(bf16[2,8,64,512]{3,2,1,0:T(8,128)(2,1)S(1)} %get-tuple-element.10, bf16[2,512,2,128]{3,1,2,0:T(8,128)(2,1)S(1)} %constant_dynamic-update-slice_fusion, f32[2,8,64]{1,0,2:T(2,128)S(1)} %copy.12), kind=kOutput, calls=%fused_computation.6 | convolution fusion | flops 134479872 | bytes 1638400 | tf_op jit(solution)/shard_map/hgqk,khd->hgqd/dot_general | solution.py:49
  (13 shorter events, 0.1 us)
Async XLA Ops:
  0.0 18.6 %copy-start = (bf16[64,16,128]{2,1,0:T(8,128)(2,1)S(1)}, bf16[64,16,128]{2,1,0:T(8,128)(2,1)}, u32[]{:S(2)}) copy-start(bf16[64,16,128]{2,1,0:T(8,128)(2,1)} %param.3) | copy-start | bytes 786436
  0.9 10.2 %collective-permute-start.4 = (bf16[2,64,2,128]{3,1,2,0:T(8,128)(2,1)S(1)}, bf16[2,64,2,128]{3,1,2,0:T(8,128)(2,1)S(1)}, u32[]{:S(2)}, u32[]{:S(2)}) collective-permute-start(bf16[2,64,2,128]{3,1,2,0:T(8,128)(2,1)S(1)} %get-tuple-element.8), channel_id=1, source_target_pairs={{0,2},{2,0},{4,6},{6,4},{8,10},{10,8},{12,14},{14,12},{1,3},{3,1},... | collective-permute-start | bytes 196616 | tf_op jit(solution)/shard_map/ppermute | solution.py:29
  3.9 9.5 %collective-permute-start.3 = (bf16[2,64,2,128]{3,1,2,0:T(8,128)(2,1)S(1)}, bf16[2,64,2,128]{3,1,2,0:T(8,128)(2,1)S(1)}, u32[]{:S(2)}, u32[]{:S(2)}) collective-permute-start(bf16[2,64,2,128]{3,1,2,0:T(8,128)(2,1)S(1)} %get-tuple-element.8), channel_id=1, source_target_pairs={{0,4},{2,6},{4,8},{6,10},{8,12},{10,14},{12,0},{14,2},{1,5},{3,7},... | collective-permute-start | bytes 196616 | tf_op jit(solution)/shard_map/ppermute | solution.py:29
  5.5 12.4 %collective-permute-start.2 = (bf16[2,64,2,128]{3,1,2,0:T(8,128)(2,1)S(1)}, bf16[2,64,2,128]{3,1,2,0:T(8,128)(2,1)S(1)}, u32[]{:S(2)}, u32[]{:S(2)}) collective-permute-start(bf16[2,64,2,128]{3,1,2,0:T(8,128)(2,1)S(1)} %get-tuple-element.8), channel_id=1, source_target_pairs={{0,6},{2,4},{4,10},{6,8},{8,14},{10,12},{12,2},{14,0},{1,7},{3,5},... | collective-permute-start | bytes 196616 | tf_op jit(solution)/shard_map/ppermute | solution.py:29
  7.0 10.9 %collective-permute-start.1 = (bf16[2,64,2,128]{3,1,2,0:T(8,128)(2,1)S(1)}, bf16[2,64,2,128]{3,1,2,0:T(8,128)(2,1)S(1)}, u32[]{:S(2)}, u32[]{:S(2)}) collective-permute-start(bf16[2,64,2,128]{3,1,2,0:T(8,128)(2,1)S(1)} %get-tuple-element.8), channel_id=1, source_target_pairs={{0,8},{2,10},{4,12},{6,14},{8,0},{10,2},{12,4},{14,6},{1,9},{3,11}... | collective-permute-start | bytes 196616 | tf_op jit(solution)/shard_map/ppermute | solution.py:29
  8.1 9.8 %collective-permute-start = (bf16[2,64,2,128]{3,1,2,0:T(8,128)(2,1)S(1)}, bf16[2,64,2,128]{3,1,2,0:T(8,128)(2,1)S(1)}, u32[]{:S(2)}, u32[]{:S(2)}) collective-permute-start(bf16[2,64,2,128]{3,1,2,0:T(8,128)(2,1)S(1)} %get-tuple-element.8), channel_id=1, source_target_pairs={{0,10},{2,8},{4,14},{6,12},{8,2},{10,0},{12,6},{14,4},{1,11},{3,9}... | collective-permute-start | bytes 196616 | tf_op jit(solution)/shard_map/ppermute | solution.py:29
  11.1 6.9 %collective-permute-start.5 = (bf16[2,64,2,128]{3,1,2,0:T(8,128)(2,1)S(1)}, bf16[2,64,2,128]{3,1,2,0:T(8,128)(2,1)S(1)}, u32[]{:S(2)}, u32[]{:S(2)}) collective-permute-start(bf16[2,64,2,128]{3,1,2,0:T(8,128)(2,1)S(1)} %get-tuple-element.8), channel_id=1, source_target_pairs={{0,12},{2,14},{4,0},{6,2},{8,4},{10,6},{12,8},{14,10},{1,13},{3,15... | collective-permute-start | bytes 196616 | tf_op jit(solution)/shard_map/ppermute | solution.py:29
  13.4 5.2 %collective-permute-start.6 = (bf16[2,64,2,128]{3,1,2,0:T(8,128)(2,1)S(1)}, bf16[2,64,2,128]{3,1,2,0:T(8,128)(2,1)S(1)}, u32[]{:S(2)}, u32[]{:S(2)}) collective-permute-start(bf16[2,64,2,128]{3,1,2,0:T(8,128)(2,1)S(1)} %get-tuple-element.8), channel_id=1, source_target_pairs={{0,14},{2,12},{4,2},{6,0},{8,6},{10,4},{12,10},{14,8},{1,15},{3,13... | collective-permute-start | bytes 196616 | tf_op jit(solution)/shard_map/ppermute | solution.py:29
